TPU v7x, 128 devices: a whole 4x4x4 slice. The times are simulated.
128 devices in a mesh: row: 8 (over x, core), col: 16 (over z, y).
Axes of the slice: x: 4, y: 4, z: 4, core: 2. Of those that a mesh axis runs over, the one named last changes fastest.
Arguments:
- hidden: bfloat16 [2048, 3584], P(('row', 'col')), may hold values from -6 to 6
- route_ids: int32 [2048, 8], P(('row', 'col')), may hold values from 0 to 127, all different within a row; in each aligned block of 16 rows (0 to 15, 16 to 31, ...) at most 2 rows name the same one
- route_scores: float32 [2048, 8], P(('row', 'col')), may hold values from 0.05 to 1
- gate_weight: bfloat16 [128, 3584, 1024], P(('row', 'col')), may hold values from -0.09375 to 0.09375
- up_weight: bfloat16 [128, 3584, 1024], P(('row', 'col')), may hold values from -0.09375 to 0.09375
- down_weight: bfloat16 [128, 1024, 3584], P(('row', 'col')), may hold values from -0.1875 to 0.1875
- queries: bfloat16 [2048, 64, 576], P(('row', 'col'))
- latent_cache: bfloat16 [2048, 128, 576], P(('row', 'col'))
- lengths: int32 [2048], P(('row', 'col')), may hold values from 1 to 128, 131072 in all
Outputs:
- expert_mix: bfloat16 [2048, 3584], P(('row', 'col'))
- context: bfloat16 [2048, 64, 512], P(('row', 'col'))
Inputs may be any that keep to these rules, and one draw needn't show every extreme that they name: `route_ids`: among the 16 sequences of one device (aligned blocks of rows), no expert is named more than 2 times, and in every draw some expert is named exactly 2 times; each row names 8 different experts. `lengths`: some sequence fills all 128 slots.
All inputs are finite; a program needn't handle non-finite values. No bound on the sum of `lengths` on one device may be relied on, other than what follows from the above.
Results may differ from a plain program's by a relative error of at most 0.013.
Values may be sent and summed in bfloat16 or wider, within the bound.
No kernel may reach another device: no remote copies, remote signals or barrier semaphores. Data moves between devices by JAX's collectives and lax.ppermute only.
A program may use at most 128 MiB of HBM per device.

v0:
```python
import jax
import jax.numpy as jnp
from jax import lax
from jax.sharding import PartitionSpec as P

LATENT = 512


SOFTMAX_SCALE = 192 ** (-0.5)


def attention(queries, latent_cache, lengths):
    scores = (
        jnp.einsum("shc,slc->shl", queries, latent_cache, preferred_element_type=jnp.float32)
        * SOFTMAX_SCALE
    )
    visible = (
        jnp.arange(latent_cache.shape[1], dtype=jnp.int32)[None, None, :] < lengths[:, None, None]
    )
    scores = jnp.where(visible, scores, jnp.float32(-1e30))
    row_max = jnp.max(scores, axis=-1, keepdims=True)
    numer = jnp.where(visible, jnp.exp(scores - row_max), jnp.float32(0.0))
    probabilities = (numer / jnp.sum(numer, axis=-1, keepdims=True)).astype(jnp.bfloat16)
    context = jnp.einsum(
        "shl,slc->shc",
        probabilities,
        latent_cache[:, :, :LATENT],
        preferred_element_type=jnp.float32,
    )
    return context.astype(jnp.bfloat16)


def expert_rows(buffer, gate_weight, up_weight, down_weight):
    model_width = buffer.shape[-1]
    row_block = buffer.reshape(-1, model_width)
    gate_part = jnp.dot(row_block, gate_weight[0], preferred_element_type=jnp.float32)
    up_part = jnp.dot(row_block, up_weight[0], preferred_element_type=jnp.float32)
    units = (jax.nn.silu(gate_part) * up_part).astype(jnp.bfloat16)
    result = jnp.dot(units, down_weight[0], preferred_element_type=jnp.float32).astype(jnp.bfloat16)
    return result.reshape(buffer.shape)


def slot_tables(targets, token_count, top_count, slot_count, hidden_rows, weights):
    placed = targets[:, None] == jnp.arange(slot_count, dtype=jnp.int32)[None, :]
    share = placed.reshape(token_count, top_count, slot_count)
    layout = jnp.any(share, axis=1).astype(jnp.bfloat16)
    outgoing = lax.dot_general(
        layout, hidden_rows, (((0,), (0,)), ((), ())), preferred_element_type=jnp.float32
    )
    mixing = jnp.sum(share.astype(jnp.float32) * weights[:, :, None], axis=1)
    return (outgoing.astype(jnp.bfloat16), mixing)


def shards(
    hidden,
    route_ids,
    route_scores,
    gate_weight,
    up_weight,
    down_weight,
    queries,
    latent_cache,
    lengths,
):
    seq_dev, model_width = hidden.shape
    top_count = route_ids.shape[1]
    row_count = lax.axis_size("row")
    col_count = lax.axis_size("col")
    experts = row_count * col_count
    capacity = max(2, 2 * seq_dev * top_count // experts)
    slot_count = experts * capacity
    combine = 2.5 * route_scores / jnp.sum(route_scores, axis=-1, keepdims=True)
    flat_ids = route_ids.reshape(-1)
    onehot = (flat_ids[:, None] == jnp.arange(experts, dtype=jnp.int32)[None, :]).astype(jnp.int32)
    before = jnp.cumsum(onehot, axis=0) - onehot
    ranking = jnp.sum(before * onehot, axis=1)
    targets = flat_ids * capacity + ranking
    outgoing, mixing = slot_tables(targets, seq_dev, top_count, slot_count, hidden, combine)
    outgoing = outgoing.reshape(experts, capacity, model_width)
    computed = expert_rows(
        lax.all_to_all(outgoing, ("row", "col"), split_axis=0, concat_axis=0, tiled=True),
        gate_weight,
        up_weight,
        down_weight,
    )
    returned = lax.all_to_all(computed, ("row", "col"), split_axis=0, concat_axis=0, tiled=True)
    returned = returned.reshape(slot_count, model_width)
    mixture = jnp.dot(
        mixing,
        returned.astype(jnp.float32),
        precision=lax.Precision.HIGHEST,
        preferred_element_type=jnp.float32,
    )
    context = attention(queries, latent_cache, lengths)
    return (mixture.astype(jnp.bfloat16), context)


def solution(mesh):
    placed = (
        P(("row", "col"), None),
        P(("row", "col"), None),
        P(("row", "col"), None),
        P(("row", "col"), None, None),
        P(("row", "col"), None, None),
        P(("row", "col"), None, None),
        P(("row", "col"), None, None),
        P(("row", "col"), None, None),
        P(("row", "col")),
    )
    return jax.shard_map(
        shards,
        mesh=mesh,
        in_specs=placed,
        out_specs=(P(("row", "col"), None), P(("row", "col"), None, None)),
        check_vma=False,
    )
```

profile of v0, /device:TPU:0, one launch (start us, length us, event | category | flops | bytes accessed | tf_op | source)
XLA Modules:
  0.0 109.5 jit_solution(14299660749054870711)
XLA Ops:
  0.6 0.0 copy-start
  0.6 0.9 copy.19
  1.5 0.1 eq.29
  1.6 0.1 fusion.30
  1.7 0.2 reduce_window_sum.11
  1.9 0.2 select_reduce_fusion.1
  2.0 0.1 reduce_sum.39
  2.1 0.1 fusion.29
  2.3 2.8 %convolution_convert_fusion = bf16[256,3584]{1,0:T(8,128)(2,1)} fusion(pred[16,256]{1,0:T(8,128)(4,1)S(1)} %fusion.29, bf16[16,3584]{1,0:T(8,128)(2,1)} %param.9), kind=kOutput, calls=%fused_computation.8 | convolution fusion | flops 30277632 | bytes 1953792 | tf_op jit(solution)/shard_map/dot_general | solution.py:47
  5.1 3.9 %reshape.60 = bf16[128,2,3584]{2,1,0:T(2,128)(2,1)S(1)} reshape(bf16[256,3584]{1,0:T(8,128)(2,1)} %convolution_convert_fusion) | data formatting | bytes 3670016 | tf_op jit(solution)/shard_map/reshape | solution.py:79
  9.0 38.2 %all_to_all.10 = bf16[128,2,3584]{2,1,0:T(2,128)(2,1)} all-to-all(bf16[128,2,3584]{2,1,0:T(2,128)(2,1)S(1)} %reshape.60), channel_id=1, replica_groups=mesh['row'=8,'col'=16] {'row','col'}, dimensions={0} | all-to-all | bytes 3670016 | tf_op jit(solution)/shard_map/all_to_all | solution.py:81
  47.2 4.1 %reshape.61 = bf16[256,3584]{1,0:T(8,128)(2,1)S(1)} reshape(bf16[128,2,3584]{2,1,0:T(2,128)(2,1)} %all_to_all.10) | data formatting | bytes 3670016 | tf_op jit(solution)/shard_map/reshape | solution.py:35
  51.3 6.1 %fusion.5 = f32[256,1024]{1,0:T(8,128)} fusion(bf16[256,3584]{1,0:T(8,128)(2,1)S(1)} %reshape.61, bf16[1,3584,1024]{2,1,0:T(8,128)(2,1)} %param.12), kind=kOutput, calls=%fused_computation.5 | convolution fusion | flops 1879048192 | bytes 10223616 | tf_op jit(solution)/shard_map/dot_general | solution.py:36
  57.4 10.8 %fusion.7 = bf16[256,3584]{1,0:T(8,128)(2,1)} fusion(bf16[1,1024,3584]{2,1,0:T(8,128)(2,1)} %param.14, bf16[256,3584]{1,0:T(8,128)(2,1)S(1)} %reshape.61, bf16[1,3584,1024]{2,1,0:T(8,128)(2,1)} %param.13, f32[256,1024]{1,0:T(8,128)} %fusion.5), kind=kOutput, calls=%fused_computation.7 | convolution fusion | flops 3760586752 | bytes 19398656 | tf_op jit(solution)/shard_map/dot_general | solution.py:39
  68.2 4.8 %reshape.62 = bf16[128,2,3584]{2,1,0:T(2,128)(2,1)} reshape(bf16[256,3584]{1,0:T(8,128)(2,1)} %fusion.7) | data formatting | bytes 3670016 | tf_op jit(solution)/shard_map/reshape | solution.py:40
  73.0 0.0 copy-start.2
  73.0 0.0 copy-start.3
  73.0 5.0 %all-to-all-start.1 = ((bf16[128,2,3584]{2,1,0:T(2,128)(2,1)}), bf16[128,2,3584]{2,1,0:T(2,128)(2,1)S(1)}, u32[]{:S(2)}, u32[]{:S(2)}) async-start(bf16[128,2,3584]{2,1,0:T(2,128)(2,1)} %reshape.62), calls=%async_computation.1 | async-start | bytes 3670016 | tf_op jit(solution)/shard_map/all_to_all | solution.py:86
  77.9 0.0 copy-done.2
  78.0 0.1 copy.21
  78.0 0.1 select_reduce_fusion
  78.2 0.0 copy-done.3
  78.2 0.1 iota_compare_fusion.2
  78.3 0.0 copy-done
  78.3 2.3 %fusion.24 = f32[16,64,128]{2,1,0:T(8,128)S(1)} fusion(bf16[16,64,576]{2,1,0:T(8,128)(2,1)S(1)} %copy-done, bf16[16,128,576]{1,2,0:T(8,128)(2,1)} %param.16, pred[16,128]{1,0:T(8,128)(4,1)S(1)} %iota_compare_fusion.2), kind=kOutput, calls=%fused_computation.19 | convolution fusion | flops 151257088 | bytes 4065280 | tf_op jit(solution)/shard_map/shc,slc->shl/dot_general | solution.py:14
  80.6 0.0 copy-start.1
  80.6 0.8 copy-done.1
  81.4 0.3 fusion.34
  81.7 4.8 %fusion.12 = bf16[16,64,512]{2,1,0:T(8,128)(2,1)} fusion(bf16[16,128,576]{1,2,0:T(8,128)(2,1)} %param.16, f32[16,64]{1,0:T(8,128)S(1)} %fusion.34, f32[16,64,128]{2,1,0:T(8,128)} %copy-done.1, pred[16,128]{1,0:T(8,128)(4,1)S(1)} %iota_compare_fusion.2), kind=kOutput, calls=%fused_computation.12 | convolution fusion | flops 135267456 | bytes 4200448 | tf_op jit(solution)/shard_map/shl,slc->shc/dot_general | solution.py:24
  86.6 18.3 %all-to-all-done.1 = bf16[128,2,3584]{2,1,0:T(2,128)(2,1)S(1)} async-done(((bf16[128,2,3584]{2,1,0:T(2,128)(2,1)}), bf16[128,2,3584]{2,1,0:T(2,128)(2,1)S(1)}, u32[]{:S(2)}, u32[]{:S(2)}) %all-to-all-start.1) | async-done | bytes 1835040 | tf_op jit(solution)/shard_map/all_to_all | solution.py:86
  104.9 1.7 %reshape.63 = bf16[256,3584]{1,0:T(8,128)(2,1)} reshape(bf16[128,2,3584]{2,1,0:T(2,128)(2,1)S(1)} %all-to-all-done.1) | data formatting | bytes 3670016 | tf_op jit(solution)/shard_map/reshape | solution.py:87
  106.6 3.0 %convolution_convert_fusion.1 = bf16[16,3584]{1,0:T(8,128)(2,1)} fusion(f32[16,256]{1,0:T(8,128)S(1)} %select_reduce_fusion, bf16[256,3584]{1,0:T(8,128)(2,1)} %reshape.63), kind=kOutput, calls=%fused_computation.9 | convolution fusion | flops 176218112 | bytes 1966080 | tf_op jit(solution)/shard_map/dot_general | solution.py:88
  (3 shorter events, 0.0 us)
Async XLA Ops:
  0.6 77.6 %copy-start = (bf16[16,64,576]{2,1,0:T(8,128)(2,1)S(1)}, bf16[16,64,576]{2,1,0:T(8,128)(2,1)}, u32[]{:S(2)}) copy-start(bf16[16,64,576]{2,1,0:T(8,128)(2,1)} %param.15) | copy-start | bytes 3538948
  73.0 5.0 %copy-start.2 = (f32[16,8]{0,1:T(8,128)S(1)}, f32[16,8]{0,1:T(8,128)}, u32[]{:S(2)}) copy-start(f32[16,8]{0,1:T(8,128)} %param.11) | copy-start | bytes 1540
  73.0 5.2 %copy-start.3 = (s32[16]{0:T(128)S(1)}, s32[16]{0:T(128)}, u32[]{:S(2)}) copy-start(s32[16]{0:T(128)} %param.17) | copy-start | bytes 196
  73.0 31.9 %all-to-all-start.1 = ((bf16[128,2,3584]{2,1,0:T(2,128)(2,1)}), bf16[128,2,3584]{2,1,0:T(2,128)(2,1)S(1)}, u32[]{:S(2)}, u32[]{:S(2)}) async-start(bf16[128,2,3584]{2,1,0:T(2,128)(2,1)} %reshape.62), calls=%async_computation.1 | async-start | bytes 3670016 | tf_op jit(solution)/shard_map/all_to_all | solution.py:86
  80.6 0.8 copy-start.1
where the time goes:
time: 110 us
  blocking collectives  38.2 us (35%)
  matrix products  29.8 us (27%)
  waiting for transfers between devices  18.3 us (17%)
  local copies, waits for them, and re-layouts  16.3 us (15%)
  starting transfers between devices  4.96 us (5%)
  other arithmetic  1.15 us (1%)
    all_to_all x1, blocking collectives, shards(): lax.all_to_all(outgoing, ('row', 'col'), split_axis=0, concat_axis=0, til...  38.2 us
    all_to_all x1, waiting for transfers between devices, shards(): lax.all_to_all(computed, ('row', 'col'), split_axis=0, concat_axis=0, til...  18.3 us
    dot_general x1, matrix products, expert_rows(): jnp.dot(units, down_weight[0], preferred_element_type=jnp.float32)  10.8 us
    dot_general x1, matrix products, expert_rows(): jnp.dot(row_block, gate_weight[0], preferred_element_type=jnp.float32)  6.11 us
    all_to_all x1, starting transfers between devices, shards(): lax.all_to_all(computed, ('row', 'col'), split_axis=0, concat_axis=0, til...  4.96 us
    dot_general x1, matrix products, attention(): jnp.einsum('shl,slc->shc', probabilities, latent_cache[:, :, :LATENT], pr...  4.82 us
    reshape x1, local copies, waits for them, and re-layouts, expert_rows(): return result.reshape(buffer.shape)  4.79 us
    reshape x1, local copies, waits for them, and re-layouts, expert_rows(): row_block = buffer.reshape(-1, model_width)  4.06 us
  transfers between devices with their start and end apart: 1, of which 1 were waited for; matrix products, arithmetic and copies ran while one was open for 7% of the time, Pallas kernels for 0%

commit v1 on v0

--- a/solution.py
+++ b/solution.py
@@ -1,6 +1,8 @@
 import jax
 import jax.numpy as jnp
 from jax import lax
+from jax.experimental import pallas as pl
+from jax.experimental.pallas import tpu as pltpu
 from jax.sharding import PartitionSpec as P
 
 LATENT = 512
@@ -30,13 +32,48 @@
     return context.astype(jnp.bfloat16)
 
 
+FF_BLOCK = 256
+
+
+def expert_kernel(rows_ref, gate_ref, up_ref, down_ref, out_ref, acc_ref):
+    step = pl.program_id(0)
+
+    @pl.when(step == 0)
+    def _():
+        acc_ref[...] = jnp.zeros_like(acc_ref)
+
+    rows = rows_ref[...]
+    gate_part = jnp.dot(rows, gate_ref[...], preferred_element_type=jnp.float32)
+    up_part = jnp.dot(rows, up_ref[...], preferred_element_type=jnp.float32)
+    units = (gate_part / (1.0 + jnp.exp(-gate_part)) * up_part).astype(jnp.bfloat16)
+    acc_ref[...] += jnp.dot(units, down_ref[...], preferred_element_type=jnp.float32)
+
+    @pl.when(step == pl.num_programs(0) - 1)
+    def _():
+        out_ref[...] = acc_ref[...].astype(out_ref.dtype)
+
+
 def expert_rows(buffer, gate_weight, up_weight, down_weight):
     model_width = buffer.shape[-1]
+    hidden_units = gate_weight.shape[-1]
     row_block = buffer.reshape(-1, model_width)
-    gate_part = jnp.dot(row_block, gate_weight[0], preferred_element_type=jnp.float32)
-    up_part = jnp.dot(row_block, up_weight[0], preferred_element_type=jnp.float32)
-    units = (jax.nn.silu(gate_part) * up_part).astype(jnp.bfloat16)
-    result = jnp.dot(units, down_weight[0], preferred_element_type=jnp.float32).astype(jnp.bfloat16)
+    row_count = row_block.shape[0]
+    result = pl.pallas_call(
+        expert_kernel,
+        grid=(hidden_units // FF_BLOCK,),
+        in_specs=[
+            pl.BlockSpec((row_count, model_width), lambda f: (0, 0)),
+            pl.BlockSpec((None, model_width, FF_BLOCK), lambda f: (0, 0, f)),
+            pl.BlockSpec((None, model_width, FF_BLOCK), lambda f: (0, 0, f)),
+            pl.BlockSpec((None, FF_BLOCK, model_width), lambda f: (0, f, 0)),
+        ],
+        out_specs=pl.BlockSpec((row_count, model_width), lambda f: (0, 0)),
+        out_shape=jax.ShapeDtypeStruct((row_count, model_width), jnp.bfloat16),
+        scratch_shapes=[pltpu.VMEM((row_count, model_width), jnp.float32)],
+        compiler_params=pltpu.CompilerParams(
+            dimension_semantics=("arbitrary",), vmem_limit_bytes=48 * 1024 * 1024
+        ),
+    )(row_block, gate_weight, up_weight, down_weight)
     return result.reshape(buffer.shape)
 
 

time: 110 us -> 105 us (0.955)
  matrix products: 29.8 us -> 12.9 us
  Pallas kernels: 0 us -> 11 us
  local copies, waits for them, and re-layouts: 16.3 us -> 17.5 us
    dot_general x2 -> x0, matrix products: 16.9 us -> none  [the longest x1 10.8 us: expert_rows(): jnp.dot(units, down_weight[0], preferred_element_type=jnp.float32)]
    pallas_call x0 -> x1, Pallas kernels: none -> 11 us  [expert_rows(): pl.pallas_call(expert_kernel, grid=(hidden_units // FF_BLOCK,), in_specs=...]
    unnamed x9 -> x11, local copies, waits for them, and re-layouts: 1.68 us -> 2.9 us
where the time goes in v1:
time: 105 us
  blocking collectives  38.2 us (36%)
  waiting for transfers between devices  18.5 us (18%)
  local copies, waits for them, and re-layouts  17.5 us (17%)
  matrix products  12.9 us (12%)
  Pallas kernels  11 us (10%)
  starting transfers between devices  4.78 us (5%)
  other arithmetic  1.15 us (1%)
    all_to_all x1, blocking collectives, shards(): lax.all_to_all(outgoing, ('row', 'col'), split_axis=0, concat_axis=0, til...  38.2 us
    all_to_all x1, waiting for transfers between devices, shards(): lax.all_to_all(computed, ('row', 'col'), split_axis=0, concat_axis=0, til...  18.5 us
    pallas_call x1, Pallas kernels, expert_rows(): pl.pallas_call(expert_kernel, grid=(hidden_units // FF_BLOCK,), in_specs=...  11 us
    dot_general x1, matrix products, attention(): jnp.einsum('shl,slc->shc', probabilities, latent_cache[:, :, :LATENT], pr...  4.82 us
    reshape x1, local copies, waits for them, and re-layouts, expert_rows(): return result.reshape(buffer.shape)  4.79 us
    all_to_all x1, starting transfers between devices, shards(): lax.all_to_all(computed, ('row', 'col'), split_axis=0, concat_axis=0, til...  4.78 us
    reshape x1, local copies, waits for them, and re-layouts, expert_rows(): row_block = buffer.reshape(-1, model_width)  4.06 us
    reshape x1, local copies, waits for them, and re-layouts, shards(): outgoing = outgoing.reshape(experts, capacity, model_width)  3.88 us
  transfers between devices with their start and end apart: 1, of which 1 were waited for; matrix products, arithmetic and copies ran while one was open for 7% of the time, Pallas kernels for 0%

profile of v1, /device:TPU:0, one launch (start us, length us, event | category | flops | bytes accessed | tf_op | source)
XLA Modules:
  0.0 104.9 jit_solution(9936075999021697481)
XLA Ops:
  0.6 0.0 copy-start
  0.6 0.9 copy.19
  1.5 0.1 eq.29
  1.6 0.1 fusion.12
  1.7 0.2 reduce_window_sum.11
  1.9 0.2 select_reduce_fusion.1
  2.0 0.1 reduce_sum.39
  2.1 0.1 fusion.11
  2.3 2.8 %convolution_convert_fusion = bf16[256,3584]{1,0:T(8,128)(2,1)} fusion(pred[16,256]{1,0:T(8,128)(4,1)S(1)} %fusion.11, bf16[16,3584]{1,0:T(8,128)(2,1)} %param.9), kind=kOutput, calls=%fused_computation.1 | convolution fusion | flops 30277632 | bytes 1953792 | tf_op jit(solution)/shard_map/dot_general | solution.py:84
  5.1 3.9 %reshape.60 = bf16[128,2,3584]{2,1,0:T(2,128)(2,1)S(1)} reshape(bf16[256,3584]{1,0:T(8,128)(2,1)} %convolution_convert_fusion) | data formatting | bytes 3670016 | tf_op jit(solution)/shard_map/reshape | solution.py:116
  9.0 38.2 %all_to_all.10 = bf16[128,2,3584]{2,1,0:T(2,128)(2,1)} all-to-all(bf16[128,2,3584]{2,1,0:T(2,128)(2,1)S(1)} %reshape.60), channel_id=1, replica_groups=mesh['row'=8,'col'=16] {'row','col'}, dimensions={0} | all-to-all | bytes 3670016 | tf_op jit(solution)/shard_map/all_to_all | solution.py:118
  47.2 4.1 %reshape.61.rows_ref = bf16[256,3584]{1,0:T(8,128)(2,1)S(1)} reshape(bf16[128,2,3584]{2,1,0:T(2,128)(2,1)} %all_to_all.10) | data formatting | bytes 3670016 | tf_op jit(solution)/shard_map/reshape | solution.py:59
  51.3 11.0 %shard_map.104 = bf16[256,3584]{1,0:T(8,128)(2,1)S(1)} custom-call(bf16[256,3584]{1,0:T(8,128)(2,1)S(1)} %reshape.61.rows_ref, bf16[1,3584,1024]{2,1,0:T(8,128)(2,1)} %gate_ref.1, bf16[1,3584,1024]{2,1,0:T(8,128)(2,1)} %up_ref.1, bf16[1,1024,3584]{2,1,0:T(8,128)(2,1)} %down_ref.1), custom_call_target="tpu_custom_call" | custom-call | tf_op jit(solution)/shard_map/pallas_call | solution.py:61
  62.3 0.0 copy-start.1
  62.3 1.2 %copy-done.1 = bf16[256,3584]{1,0:T(8,128)(2,1)} copy-done((bf16[256,3584]{1,0:T(8,128)(2,1)}, bf16[256,3584]{1,0:T(8,128)(2,1)S(1)}, u32[]{:S(2)}) %copy-start.1) | copy-done | bytes 1835032
  63.5 4.8 %reshape.62 = bf16[128,2,3584]{2,1,0:T(2,128)(2,1)} reshape(bf16[256,3584]{1,0:T(8,128)(2,1)} %copy-done.1) | data formatting | bytes 3670016 | tf_op jit(solution)/shard_map/reshape | solution.py:77
  68.3 0.0 copy-start.3
  68.3 4.8 %all-to-all-start.1 = ((bf16[128,2,3584]{2,1,0:T(2,128)(2,1)}), bf16[128,2,3584]{2,1,0:T(2,128)(2,1)S(1)}, u32[]{:S(2)}, u32[]{:S(2)}) async-start(bf16[128,2,3584]{2,1,0:T(2,128)(2,1)} %reshape.62), calls=%async_computation.1 | async-start | bytes 3670016 | tf_op jit(solution)/shard_map/all_to_all | solution.py:123
  73.1 0.0 copy-done.3
  73.1 0.1 copy.21
  73.2 0.1 select_reduce_fusion
  73.3 0.0 copy-done.4
  73.4 0.1 iota_compare_fusion.2
  73.4 0.0 copy-done
  73.4 2.3 %fusion.9 = f32[16,64,128]{2,1,0:T(8,128)S(1)} fusion(bf16[16,64,576]{2,1,0:T(8,128)(2,1)S(1)} %copy-done, bf16[16,128,576]{1,2,0:T(8,128)(2,1)} %param.16, pred[16,128]{1,0:T(8,128)(4,1)S(1)} %iota_compare_fusion.2), kind=kOutput, calls=%fused_computation.10 | convolution fusion | flops 151257088 | bytes 4065280 | tf_op jit(solution)/shard_map/shc,slc->shl/dot_general | solution.py:16
  75.7 0.0 copy-start.2
  75.8 0.8 copy-done.2
  76.6 0.3 fusion.15
  76.9 4.8 %fusion.3 = bf16[16,64,512]{2,1,0:T(8,128)(2,1)} fusion(bf16[16,128,576]{1,2,0:T(8,128)(2,1)} %param.16, f32[16,64]{1,0:T(8,128)S(1)} %fusion.15, f32[16,64,128]{2,1,0:T(8,128)} %copy-done.2, pred[16,128]{1,0:T(8,128)(4,1)S(1)} %iota_compare_fusion.2), kind=kOutput, calls=%fused_computation.5 | convolution fusion | flops 135267456 | bytes 4200448 | tf_op jit(solution)/shard_map/shl,slc->shc/dot_general | solution.py:26
  81.7 18.5 %all-to-all-done.1 = bf16[128,2,3584]{2,1,0:T(2,128)(2,1)S(1)} async-done(((bf16[128,2,3584]{2,1,0:T(2,128)(2,1)}), bf16[128,2,3584]{2,1,0:T(2,128)(2,1)S(1)}, u32[]{:S(2)}, u32[]{:S(2)}) %all-to-all-start.1) | async-done | bytes 1835040 | tf_op jit(solution)/shard_map/all_to_all | solution.py:123
  100.2 1.7 %reshape.63 = bf16[256,3584]{1,0:T(8,128)(2,1)} reshape(bf16[128,2,3584]{2,1,0:T(2,128)(2,1)S(1)} %all-to-all-done.1) | data formatting | bytes 3670016 | tf_op jit(solution)/shard_map/reshape | solution.py:124
  101.9 3.0 %convolution_convert_fusion.1 = bf16[16,3584]{1,0:T(8,128)(2,1)} fusion(f32[16,256]{1,0:T(8,128)S(1)} %select_reduce_fusion, bf16[256,3584]{1,0:T(8,128)(2,1)} %reshape.63), kind=kOutput, calls=%fused_computation.2 | convolution fusion | flops 176218112 | bytes 1966080 | tf_op jit(solution)/shard_map/dot_general | solution.py:125
  (4 shorter events, 0.0 us)
Async XLA Ops:
  0.6 72.8 %copy-start = (bf16[16,64,576]{2,1,0:T(8,128)(2,1)S(1)}, bf16[16,64,576]{2,1,0:T(8,128)(2,1)}, u32[]{:S(2)}) copy-start(bf16[16,64,576]{2,1,0:T(8,128)(2,1)} %param.15) | copy-start | bytes 3538948
  62.3 1.2 %copy-start.1 = (bf16[256,3584]{1,0:T(8,128)(2,1)}, bf16[256,3584]{1,0:T(8,128)(2,1)S(1)}, u32[]{:S(2)}) copy-start(bf16[256,3584]{1,0:T(8,128)(2,1)S(1)} %shard_map.104) | copy-start | bytes 5505028
  68.3 4.8 %copy-start.3 = (f32[16,8]{0,1:T(8,128)S(1)}, f32[16,8]{0,1:T(8,128)}, u32[]{:S(2)}) copy-start(f32[16,8]{0,1:T(8,128)} %param.11) | copy-start | bytes 1540
  68.3 5.0 %copy-start.4 = (s32[16]{0:T(128)S(1)}, s32[16]{0:T(128)}, u32[]{:S(2)}) copy-start(s32[16]{0:T(128)} %param.17) | copy-start | bytes 196
  68.3 31.9 %all-to-all-start.1 = ((bf16[128,2,3584]{2,1,0:T(2,128)(2,1)}), bf16[128,2,3584]{2,1,0:T(2,128)(2,1)S(1)}, u32[]{:S(2)}, u32[]{:S(2)}) async-start(bf16[128,2,3584]{2,1,0:T(2,128)(2,1)} %reshape.62), calls=%async_computation.1 | async-start | bytes 3670016 | tf_op jit(solution)/shard_map/all_to_all | solution.py:123
  75.7 0.8 copy-start.2

commit v2 on v1

v2 whole, which is shorter than its diff:
```python
import jax
import jax.numpy as jnp
from jax import lax
from jax.experimental import pallas as pl
from jax.experimental.pallas import tpu as pltpu
from jax.sharding import PartitionSpec as P

LATENT = 512


SOFTMAX_SCALE = 192 ** (-0.5)


def attention(queries, latent_cache, lengths):
    scores = (
        jnp.einsum("shc,slc->shl", queries, latent_cache, preferred_element_type=jnp.float32)
        * SOFTMAX_SCALE
    )
    visible = (
        jnp.arange(latent_cache.shape[1], dtype=jnp.int32)[None, None, :] < lengths[:, None, None]
    )
    scores = jnp.where(visible, scores, jnp.float32(-1e30))
    row_max = jnp.max(scores, axis=-1, keepdims=True)
    numer = jnp.where(visible, jnp.exp(scores - row_max), jnp.float32(0.0))
    probabilities = (numer / jnp.sum(numer, axis=-1, keepdims=True)).astype(jnp.bfloat16)
    context = jnp.einsum(
        "shl,slc->shc",
        probabilities,
        latent_cache[:, :, :LATENT],
        preferred_element_type=jnp.float32,
    )
    return context.astype(jnp.bfloat16)


FF_BLOCK = 256


def expert_kernel(rows_ref, gate_ref, up_ref, down_ref, out_ref, acc_ref):
    step = pl.program_id(0)
    capacity = rows_ref.shape[1]
    sources = rows_ref.shape[0]

    @pl.when(step == 0)
    def _():
        acc_ref[...] = jnp.zeros_like(acc_ref)

    for slot in range(capacity):
        rows = rows_ref[:, slot, :]
        gate_part = jnp.dot(rows, gate_ref[...], preferred_element_type=jnp.float32)
        up_part = jnp.dot(rows, up_ref[...], preferred_element_type=jnp.float32)
        units = (gate_part / (1.0 + jnp.exp(-gate_part)) * up_part).astype(jnp.bfloat16)
        acc_ref[slot] += jnp.dot(units, down_ref[...], preferred_element_type=jnp.float32)

    @pl.when(step == pl.num_programs(0) - 1)
    def _():
        for slot in range(capacity):
            out_ref[:, slot, :] = acc_ref[slot].astype(out_ref.dtype)


def expert_rows(buffer, gate_weight, up_weight, down_weight):
    sources, capacity, model_width = buffer.shape
    hidden_units = gate_weight.shape[-1]
    return pl.pallas_call(
        expert_kernel,
        grid=(hidden_units // FF_BLOCK,),
        in_specs=[
            pl.BlockSpec(buffer.shape, lambda f: (0, 0, 0)),
            pl.BlockSpec((None, model_width, FF_BLOCK), lambda f: (0, 0, f)),
            pl.BlockSpec((None, model_width, FF_BLOCK), lambda f: (0, 0, f)),
            pl.BlockSpec((None, FF_BLOCK, model_width), lambda f: (0, f, 0)),
        ],
        out_specs=pl.BlockSpec(buffer.shape, lambda f: (0, 0, 0)),
        out_shape=jax.ShapeDtypeStruct(buffer.shape, jnp.bfloat16),
        scratch_shapes=[pltpu.VMEM((capacity, sources, model_width), jnp.float32)],
        compiler_params=pltpu.CompilerParams(
            dimension_semantics=("arbitrary",), vmem_limit_bytes=48 * 1024 * 1024
        ),
    )(buffer, gate_weight, up_weight, down_weight)


def dispatch_kernel(layout_ref, hidden_ref, out_ref):
    hidden_rows = hidden_ref[...]
    for slot in range(out_ref.shape[1]):
        placed = jnp.dot(layout_ref[slot], hidden_rows, preferred_element_type=jnp.float32)
        out_ref[:, slot, :] = placed.astype(out_ref.dtype)


def combine_kernel(mixing_ref, returned_ref, out_ref):
    total = jnp.zeros(out_ref.shape, jnp.float32)
    for slot in range(returned_ref.shape[1]):
        rows = returned_ref[:, slot, :]
        weights = mixing_ref[slot]
        high = weights.astype(jnp.bfloat16)
        rest = weights - high.astype(jnp.float32)
        middle = rest.astype(jnp.bfloat16)
        low = (rest - middle.astype(jnp.float32)).astype(jnp.bfloat16)
        for part in (high, middle, low):
            total += jnp.dot(part, rows, preferred_element_type=jnp.float32)
    out_ref[...] = total.astype(out_ref.dtype)


def shards(
    hidden,
    route_ids,
    route_scores,
    gate_weight,
    up_weight,
    down_weight,
    queries,
    latent_cache,
    lengths,
):
    seq_dev, model_width = hidden.shape
    top_count = route_ids.shape[1]
    row_count = lax.axis_size("row")
    col_count = lax.axis_size("col")
    experts = row_count * col_count
    capacity = max(2, 2 * seq_dev * top_count // experts)
    combine = 2.5 * route_scores / jnp.sum(route_scores, axis=-1, keepdims=True)
    flat_ids = route_ids.reshape(-1)
    onehot = (flat_ids[:, None] == jnp.arange(experts, dtype=jnp.int32)[None, :]).astype(jnp.int32)
    before = jnp.cumsum(onehot, axis=0) - onehot
    ranking = jnp.sum(before * onehot, axis=1)
    share = (
        (onehot[None, :, :] > 0)
        & (ranking[None, :, None] == jnp.arange(capacity, dtype=jnp.int32)[:, None, None])
    ).reshape(capacity, seq_dev, top_count, experts)
    layout = jnp.swapaxes(jnp.any(share, axis=2), 1, 2).astype(jnp.bfloat16)
    mixing = jnp.sum(share.astype(jnp.float32) * combine[None, :, :, None], axis=2)
    outgoing = pl.pallas_call(
        dispatch_kernel,
        out_shape=jax.ShapeDtypeStruct((experts, capacity, model_width), jnp.bfloat16),
    )(layout, hidden)
    computed = expert_rows(
        lax.all_to_all(outgoing, ("row", "col"), split_axis=0, concat_axis=0, tiled=True),
        gate_weight,
        up_weight,
        down_weight,
    )
    returned = lax.all_to_all(computed, ("row", "col"), split_axis=0, concat_axis=0, tiled=True)
    mixture = pl.pallas_call(
        combine_kernel,
        out_shape=jax.ShapeDtypeStruct((seq_dev, model_width), jnp.bfloat16),
    )(mixing, returned)
    context = attention(queries, latent_cache, lengths)
    return (mixture, context)


def solution(mesh):
    placed = (
        P(("row", "col"), None),
        P(("row", "col"), None),
        P(("row", "col"), None),
        P(("row", "col"), None, None),
        P(("row", "col"), None, None),
        P(("row", "col"), None, None),
        P(("row", "col"), None, None),
        P(("row", "col"), None, None),
        P(("row", "col")),
    )
    return jax.shard_map(
        shards,
        mesh=mesh,
        in_specs=placed,
        out_specs=(P(("row", "col"), None), P(("row", "col"), None, None)),
        check_vma=False,
    )
```

time: 105 us -> 112 us (1.067)
  Pallas kernels: 11 us -> 36.7 us
  local copies, waits for them, and re-layouts: 17.5 us -> 3.91 us
  matrix products: 12.9 us -> 7.15 us
    pallas_call x1, Pallas kernels: 11 us -> 26.8 us  [expert_rows(): pl.pallas_call(expert_kernel, grid=(hidden_units // FF_BLOCK,), in_specs=...]
    reshape x4 -> x0, local copies, waits for them, and re-layouts: 14.4 us -> none  [the longest x1 4.79 us: expert_rows(): return result.reshape(buffer.shape)]
    pallas_call x0 -> x2, Pallas kernels: none -> 9.82 us  [the longest x1 6.75 us: shards(): pl.pallas_call(combine_kernel, out_shape=jax.ShapeDtypeStruct((seq_dev, m...]
    dot_general x2 -> x0, matrix products: 5.8 us -> none  [the longest x1 2.97 us: shards(): jnp.dot(mixing, returned.astype(jnp.float32), precision=lax.Precision.HIG...]
  transfers between devices with their start and end apart: 1 -> 1, of which waited for: 1 -> 1; matrix products, arithmetic and copies ran while one was open for 7% -> 8% of each run, Pallas kernels for 0% -> 0%
where the time goes in v2:
time: 112 us; the launch traced here: 111 us
  blocking collectives  38.3 us (34%)
  Pallas kernels  36.7 us (33%)
  waiting for transfers between devices  17.7 us (16%)
  matrix products  7.15 us (6%)
  starting transfers between devices  4.96 us (4%)
  local copies, waits for them, and re-layouts  3.91 us (3%)
  other arithmetic  1.85 us (2%)
    all_to_all x1, blocking collectives, shards(): lax.all_to_all(outgoing, ('row', 'col'), split_axis=0, concat_axis=0, til...  38.3 us
    pallas_call x1, Pallas kernels, expert_rows(): pl.pallas_call(expert_kernel, grid=(hidden_units // FF_BLOCK,), in_specs=...  26.8 us
    all_to_all x1, waiting for transfers between devices, shards(): lax.all_to_all(computed, ('row', 'col'), split_axis=0, concat_axis=0, til...  17.7 us
    pallas_call x1, Pallas kernels, shards(): pl.pallas_call(combine_kernel, out_shape=jax.ShapeDtypeStruct((seq_dev, m...  6.75 us
    all_to_all x1, starting transfers between devices, shards(): lax.all_to_all(computed, ('row', 'col'), split_axis=0, concat_axis=0, til...  4.96 us
    dot_general x1, matrix products, attention(): jnp.einsum('shl,slc->shc', probabilities, latent_cache[:, :, :LATENT], pr...  4.82 us
    pallas_call x1, Pallas kernels, shards(): pl.pallas_call(dispatch_kernel, out_shape=jax.ShapeDtypeStruct((experts,...  3.07 us
    unnamed x11, local copies, waits for them, and re-layouts  2.93 us
  transfers between devices with their start and end apart: 1, of which 1 were waited for; matrix products, arithmetic and copies ran while one was open for 8% of the time, Pallas kernels for 0%

profile of v2, /device:TPU:0, one launch (start us, length us, event | category | flops | bytes accessed | tf_op | source)
XLA Modules:
  0.0 111.3 jit_solution(15958971365996282588)
XLA Ops:
  0.6 0.0 copy-start
  0.6 0.9 copy.19
  1.5 0.1 eq.48
  1.6 0.1 convert_compare_fusion
  1.7 0.1 fusion.12
  1.8 0.2 reduce_window_sum.11
  2.0 0.2 select_reduce_fusion
  2.1 0.1 eq.52
  2.2 0.1 and_reduce_fusion
  2.4 0.7 copy.22
  3.1 3.1 %shard_map.104 = bf16[128,2,3584]{2,1,0:T(2,128)(2,1)} custom-call(bf16[2,128,16]{2,1,0:T(8,128)(2,1)} %bitcast.5, bf16[16,3584]{1,0:T(8,128)(2,1)} %hidden_ref.1), custom_call_target="tpu_custom_call" | custom-call | tf_op jit(solution)/shard_map/pallas_call | solution.py:130
  6.2 38.3 %all_to_all.10.rows_ref = bf16[128,2,3584]{2,1,0:T(2,128)(2,1)S(1)} all-to-all(bf16[128,2,3584]{2,1,0:T(2,128)(2,1)} %shard_map.104), channel_id=1, replica_groups=mesh['row'=8,'col'=16] {'row','col'}, dimensions={0} | all-to-all | bytes 3670016 | tf_op jit(solution)/shard_map/all_to_all | solution.py:135
  44.5 26.8 %shard_map.105 = bf16[128,2,3584]{2,1,0:T(2,128)(2,1)} custom-call(bf16[128,2,3584]{2,1,0:T(2,128)(2,1)S(1)} %all_to_all.10.rows_ref, bf16[1,3584,1024]{2,1,0:T(8,128)(2,1)} %gate_ref.1, bf16[1,3584,1024]{2,1,0:T(8,128)(2,1)} %up_ref.1, bf16[1,1024,3584]{2,1,0:T(8,128)(2,1)} %down_ref.1), custom_call_target="tpu_custom_call" | custom-call | tf_op jit(solution)/shard_map/pallas_call | solution.py:63
  71.3 0.0 copy-start.3
  71.3 0.0 copy-start.4
  71.3 5.0 %all-to-all-start.1 = ((bf16[128,2,3584]{2,1,0:T(2,128)(2,1)}), bf16[128,2,3584]{2,1,0:T(2,128)(2,1)S(1)}, u32[]{:S(2)}, u32[]{:S(2)}) async-start(bf16[128,2,3584]{2,1,0:T(2,128)(2,1)} %shard_map.105), calls=%async_computation.1 | async-start | bytes 3670016 | tf_op jit(solution)/shard_map/all_to_all | solution.py:140
  76.3 0.0 copy-done.3
  76.3 0.1 copy.21
  76.4 0.7 fusion.11.mixing_ref
  77.2 0.0 copy-done.4
  77.2 0.1 iota_compare_fusion.3
  77.2 0.0 copy-done
  77.2 2.3 %fusion.9 = f32[16,64,128]{2,1,0:T(8,128)S(1)} fusion(bf16[16,64,576]{2,1,0:T(8,128)(2,1)S(1)} %copy-done, bf16[16,128,576]{1,2,0:T(8,128)(2,1)} %param.16, pred[16,128]{1,0:T(8,128)(4,1)S(1)} %iota_compare_fusion.3), kind=kOutput, calls=%fused_computation.8 | convolution fusion | flops 151257088 | bytes 4065280 | tf_op jit(solution)/shard_map/shc,slc->shl/dot_general | solution.py:16
  79.6 0.0 copy-start.2
  79.6 0.8 copy-done.2
  80.4 0.3 fusion.15
  80.7 4.8 %fusion.3 = bf16[16,64,512]{2,1,0:T(8,128)(2,1)} fusion(bf16[16,128,576]{1,2,0:T(8,128)(2,1)} %param.16, f32[16,64]{1,0:T(8,128)S(1)} %fusion.15, f32[16,64,128]{2,1,0:T(8,128)} %copy-done.2, pred[16,128]{1,0:T(8,128)(4,1)S(1)} %iota_compare_fusion.3), kind=kOutput, calls=%fused_computation.3 | convolution fusion | flops 135267456 | bytes 4200448 | tf_op jit(solution)/shard_map/shl,slc->shc/dot_general | solution.py:26
  85.6 17.7 %all-to-all-done.1.returned_ref = bf16[128,2,3584]{2,1,0:T(2,128)(2,1)S(1)} async-done(((bf16[128,2,3584]{2,1,0:T(2,128)(2,1)}), bf16[128,2,3584]{2,1,0:T(2,128)(2,1)S(1)}, u32[]{:S(2)}, u32[]{:S(2)}) %all-to-all-start.1) | async-done | bytes 1835040 | tf_op jit(solution)/shard_map/all_to_all | solution.py:140
  103.3 0.0 copy-start.1
  103.3 1.3 %copy-done.1 = bf16[128,2,3584]{2,1,0:T(2,128)(2,1)} copy-done((bf16[128,2,3584]{2,1,0:T(2,128)(2,1)}, bf16[128,2,3584]{2,1,0:T(2,128)(2,1)S(1)}, u32[]{:S(2)}) %copy-start.1) | copy-done | bytes 1835032
  104.5 6.7 %shard_map.106 = bf16[16,3584]{1,0:T(8,128)(2,1)} custom-call(f32[2,16,128]{2,1,0:T(8,128)} %fusion.11.mixing_ref, bf16[128,2,3584]{2,1,0:T(2,128)(2,1)} %copy-done.1), custom_call_target="tpu_custom_call" | custom-call | tf_op jit(solution)/shard_map/pallas_call | solution.py:141
  (4 shorter events, 0.1 us)
Async XLA Ops:
  0.6 76.6 %copy-start = (bf16[16,64,576]{2,1,0:T(8,128)(2,1)S(1)}, bf16[16,64,576]{2,1,0:T(8,128)(2,1)}, u32[]{:S(2)}) copy-start(bf16[16,64,576]{2,1,0:T(8,128)(2,1)} %param.15) | copy-start | bytes 3538948
  71.3 5.0 %copy-start.3 = (f32[16,8]{0,1:T(8,128)S(1)}, f32[16,8]{0,1:T(8,128)}, u32[]{:S(2)}) copy-start(f32[16,8]{0,1:T(8,128)} %param.11) | copy-start | bytes 1540
  71.3 5.8 %copy-start.4 = (s32[16]{0:T(128)S(1)}, s32[16]{0:T(128)}, u32[]{:S(2)}) copy-start(s32[16]{0:T(128)} %param.17) | copy-start | bytes 196
  71.3 31.9 %all-to-all-start.1 = ((bf16[128,2,3584]{2,1,0:T(2,128)(2,1)}), bf16[128,2,3584]{2,1,0:T(2,128)(2,1)S(1)}, u32[]{:S(2)}, u32[]{:S(2)}) async-start(bf16[128,2,3584]{2,1,0:T(2,128)(2,1)} %shard_map.105), calls=%async_computation.1 | async-start | bytes 3670016 | tf_op jit(solution)/shard_map/all_to_all | solution.py:140
  79.6 0.8 copy-start.2
  103.3 1.3 %copy-start.1 = (bf16[128,2,3584]{2,1,0:T(2,128)(2,1)}, bf16[128,2,3584]{2,1,0:T(2,128)(2,1)S(1)}, u32[]{:S(2)}) copy-start(bf16[128,2,3584]{2,1,0:T(2,128)(2,1)S(1)} %all-to-all-done.1.returned_ref) | copy-start | bytes 5505028

commit v3 on v2

--- a/solution.py
+++ b/solution.py
@@ -35,17 +35,18 @@
 FF_BLOCK = 256
 
 
-def expert_kernel(rows_ref, gate_ref, up_ref, down_ref, out_ref, acc_ref):
+def expert_kernel(rows_ref, gate_ref, up_ref, down_ref, out_ref, slots_ref, acc_ref):
     step = pl.program_id(0)
     capacity = rows_ref.shape[1]
-    sources = rows_ref.shape[0]
 
     @pl.when(step == 0)
     def _():
+        for slot in range(capacity):
+            slots_ref[slot] = rows_ref[:, slot, :]
         acc_ref[...] = jnp.zeros_like(acc_ref)
 
     for slot in range(capacity):
-        rows = rows_ref[:, slot, :]
+        rows = slots_ref[slot]
         gate_part = jnp.dot(rows, gate_ref[...], preferred_element_type=jnp.float32)
         up_part = jnp.dot(rows, up_ref[...], preferred_element_type=jnp.float32)
         units = (gate_part / (1.0 + jnp.exp(-gate_part)) * up_part).astype(jnp.bfloat16)
@@ -71,7 +72,10 @@
         ],
         out_specs=pl.BlockSpec(buffer.shape, lambda f: (0, 0, 0)),
         out_shape=jax.ShapeDtypeStruct(buffer.shape, jnp.bfloat16),
-        scratch_shapes=[pltpu.VMEM((capacity, sources, model_width), jnp.float32)],
+        scratch_shapes=[
+            pltpu.VMEM((capacity, sources, model_width), jnp.bfloat16),
+            pltpu.VMEM((capacity, sources, model_width), jnp.float32),
+        ],
         compiler_params=pltpu.CompilerParams(
             dimension_semantics=("arbitrary",), vmem_limit_bytes=48 * 1024 * 1024
         ),
@@ -83,20 +87,6 @@
     for slot in range(out_ref.shape[1]):
         placed = jnp.dot(layout_ref[slot], hidden_rows, preferred_element_type=jnp.float32)
         out_ref[:, slot, :] = placed.astype(out_ref.dtype)
-
-
-def combine_kernel(mixing_ref, returned_ref, out_ref):
-    total = jnp.zeros(out_ref.shape, jnp.float32)
-    for slot in range(returned_ref.shape[1]):
-        rows = returned_ref[:, slot, :]
-        weights = mixing_ref[slot]
-        high = weights.astype(jnp.bfloat16)
-        rest = weights - high.astype(jnp.float32)
-        middle = rest.astype(jnp.bfloat16)
-        low = (rest - middle.astype(jnp.float32)).astype(jnp.bfloat16)
-        for part in (high, middle, low):
-            total += jnp.dot(part, rows, preferred_element_type=jnp.float32)
-    out_ref[...] = total.astype(out_ref.dtype)
 
 
 def shards(
@@ -138,10 +128,14 @@
         down_weight,
     )
     returned = lax.all_to_all(computed, ("row", "col"), split_axis=0, concat_axis=0, tiled=True)
-    mixture = pl.pallas_call(
-        combine_kernel,
-        out_shape=jax.ShapeDtypeStruct((seq_dev, model_width), jnp.bfloat16),
-    )(mixing, returned)
+    mixing = jnp.transpose(mixing, (1, 2, 0)).reshape(seq_dev, experts * capacity)
+    returned = returned.reshape(experts * capacity, model_width)
+    mixture = jnp.dot(
+        mixing,
+        returned.astype(jnp.float32),
+        precision=lax.Precision.HIGHEST,
+        preferred_element_type=jnp.float32,
+    ).astype(jnp.bfloat16)
     context = attention(queries, latent_cache, lengths)
     return (mixture, context)
 

time: 112 us -> 95.7 us (0.85)
  Pallas kernels: 36.7 us -> 20.5 us
  matrix products: 7.15 us -> 8.61 us
  local copies, waits for them, and re-layouts: 3.91 us -> 2.66 us
    pallas_call x1, Pallas kernels: 26.8 us -> 17.5 us  [expert_rows(): pl.pallas_call(expert_kernel, grid=(hidden_units // FF_BLOCK,), in_specs=...]
    pallas_call x1 -> x0, Pallas kernels: 6.75 us -> none  [shards(): pl.pallas_call(combine_kernel, out_shape=jax.ShapeDtypeStruct((seq_dev, m...]
    dot_general x0 -> x1, matrix products: none -> 1.48 us  [shards(): jnp.dot(mixing, returned.astype(jnp.float32), precision=lax.Precision.HIG...]
    unnamed x11 -> x9, local copies, waits for them, and re-layouts: 2.93 us -> 1.68 us
where the time goes in v3:
time: 95.7 us; the launch traced here: 95.4 us
  blocking collectives  38.3 us (40%)
  Pallas kernels  20.5 us (21%)
  waiting for transfers between devices  18.3 us (19%)
  matrix products  8.61 us (9%)
  starting transfers between devices  4.96 us (5%)
  local copies, waits for them, and re-layouts  2.66 us (3%)
  other arithmetic  1.26 us (1%)
    all_to_all x1, blocking collectives, shards(): lax.all_to_all(outgoing, ('row', 'col'), split_axis=0, concat_axis=0, til...  38.3 us
    all_to_all x1, waiting for transfers between devices, shards(): lax.all_to_all(computed, ('row', 'col'), split_axis=0, concat_axis=0, til...  18.3 us
    pallas_call x1, Pallas kernels, expert_rows(): pl.pallas_call(expert_kernel, grid=(hidden_units // FF_BLOCK,), in_specs=...  17.5 us
    all_to_all x1, starting transfers between devices, shards(): lax.all_to_all(computed, ('row', 'col'), split_axis=0, concat_axis=0, til...  4.96 us
    dot_general x1, matrix products, attention(): jnp.einsum('shl,slc->shc', probabilities, latent_cache[:, :, :LATENT], pr...  4.82 us
    pallas_call x1, Pallas kernels, shards(): pl.pallas_call(dispatch_kernel, out_shape=jax.ShapeDtypeStruct((experts,...  3.07 us
    dot_general x1, matrix products, attention(): jnp.einsum('shc,slc->shl', queries, latent_cache, preferred_element_type=...  2.31 us
  transfers between devices with their start and end apart: 1, of which 1 were waited for; matrix products, arithmetic and copies ran while one was open for 8% of the time, Pallas kernels for 0%

profile of v3, /device:TPU:0, one launch (start us, length us, event | category | flops | bytes accessed | tf_op | source)
XLA Modules:
  0.0 95.4 jit_solution(11374405619635651552)
XLA Ops:
  0.6 0.0 copy-start
  0.6 0.9 copy.21
  1.5 0.1 eq.48
  1.6 0.1 convert_compare_fusion
  1.7 0.1 fusion.14
  1.8 0.2 reduce_window_sum.11
  2.0 0.2 select_reduce_fusion
  2.1 0.1 eq.52
  2.2 0.1 and_reduce_fusion
  2.4 0.7 copy.24
  3.1 3.1 %shard_map.104 = bf16[128,2,3584]{2,1,0:T(2,128)(2,1)} custom-call(bf16[2,128,16]{2,1,0:T(8,128)(2,1)} %bitcast.12, bf16[16,3584]{1,0:T(8,128)(2,1)} %hidden_ref.1), custom_call_target="tpu_custom_call" | custom-call | tf_op jit(solution)/shard_map/pallas_call | solution.py:120
  6.2 38.3 %all_to_all.10.rows_ref = bf16[128,2,3584]{2,1,0:T(2,128)(2,1)S(1)} all-to-all(bf16[128,2,3584]{2,1,0:T(2,128)(2,1)} %shard_map.104), channel_id=1, replica_groups=mesh['row'=8,'col'=16] {'row','col'}, dimensions={0} | all-to-all | bytes 3670016 | tf_op jit(solution)/shard_map/all_to_all | solution.py:125
  44.5 17.5 %shard_map.105 = bf16[128,2,3584]{2,1,0:T(2,128)(2,1)} custom-call(bf16[128,2,3584]{2,1,0:T(2,128)(2,1)S(1)} %all_to_all.10.rows_ref, bf16[1,3584,1024]{2,1,0:T(8,128)(2,1)} %gate_ref.1, bf16[1,3584,1024]{2,1,0:T(8,128)(2,1)} %up_ref.1, bf16[1,1024,3584]{2,1,0:T(8,128)(2,1)} %down_ref.1), custom_call_target="tpu_custom_call" | custom-call | tf_op jit(solution)/shard_map/pallas_call | solution.py:64
  62.0 0.0 copy-start.2
  62.0 0.0 copy-start.3
  62.0 5.0 %all-to-all-start.1 = ((bf16[128,2,3584]{2,1,0:T(2,128)(2,1)}), bf16[128,2,3584]{2,1,0:T(2,128)(2,1)S(1)}, u32[]{:S(2)}, u32[]{:S(2)}) async-start(bf16[128,2,3584]{2,1,0:T(2,128)(2,1)} %shard_map.105), calls=%async_computation.1 | async-start | bytes 3670016 | tf_op jit(solution)/shard_map/all_to_all | solution.py:130
  66.9 0.0 copy-done.2
  67.0 0.1 copy.23
  67.1 0.1 fusion.13
  67.2 0.0 copy-done.3
  67.2 0.1 iota_compare_fusion.3
  67.3 0.0 copy-done
  67.3 2.3 %fusion.11 = f32[16,64,128]{2,1,0:T(8,128)S(1)} fusion(bf16[16,64,576]{2,1,0:T(8,128)(2,1)S(1)} %copy-done, bf16[16,128,576]{1,2,0:T(8,128)(2,1)} %param.16, pred[16,128]{1,0:T(8,128)(4,1)S(1)} %iota_compare_fusion.3), kind=kOutput, calls=%fused_computation.11 | convolution fusion | flops 151257088 | bytes 4065280 | tf_op jit(solution)/shard_map/shc,slc->shl/dot_general | solution.py:16
  69.6 0.0 copy-start.1
  69.6 0.8 copy-done.1
  70.4 0.3 fusion.18
  70.8 4.8 %fusion.5 = bf16[16,64,512]{2,1,0:T(8,128)(2,1)} fusion(bf16[16,128,576]{1,2,0:T(8,128)(2,1)} %param.16, f32[16,64]{1,0:T(8,128)S(1)} %fusion.18, f32[16,64,128]{2,1,0:T(8,128)} %copy-done.1, pred[16,128]{1,0:T(8,128)(4,1)S(1)} %iota_compare_fusion.3), kind=kOutput, calls=%fused_computation.6 | convolution fusion | flops 135267456 | bytes 4200448 | tf_op jit(solution)/shard_map/shl,slc->shc/dot_general | solution.py:26
  75.6 18.3 %all-to-all-done.1 = bf16[128,2,3584]{2,1,0:T(2,128)(2,1)S(1)} async-done(((bf16[128,2,3584]{2,1,0:T(2,128)(2,1)}), bf16[128,2,3584]{2,1,0:T(2,128)(2,1)S(1)}, u32[]{:S(2)}, u32[]{:S(2)}) %all-to-all-start.1) | async-done | bytes 1835040 | tf_op jit(solution)/shard_map/all_to_all | solution.py:130
  93.9 1.5 %fusion.1 = bf16[16,3584]{1,0:T(8,128)(2,1)} fusion(bf16[128,2,3584]{2,1,0:T(2,128)(2,1)S(1)} %all-to-all-done.1, f32[2,16,128]{2,1,0:T(8,128)S(1)} %fusion.13), kind=kOutput, calls=%fused_computation.2 | convolution fusion | flops 176218112 | bytes 1966080 | tf_op jit(solution)/shard_map/dot_general | solution.py:133
  (4 shorter events, 0.1 us)
Async XLA Ops:
  0.6 66.7 %copy-start = (bf16[16,64,576]{2,1,0:T(8,128)(2,1)S(1)}, bf16[16,64,576]{2,1,0:T(8,128)(2,1)}, u32[]{:S(2)}) copy-start(bf16[16,64,576]{2,1,0:T(8,128)(2,1)} %param.15) | copy-start | bytes 3538948
  62.0 5.0 %copy-start.2 = (f32[16,8]{0,1:T(8,128)S(1)}, f32[16,8]{0,1:T(8,128)}, u32[]{:S(2)}) copy-start(f32[16,8]{0,1:T(8,128)} %param.11) | copy-start | bytes 1540
  62.0 5.2 %copy-start.3 = (s32[16]{0:T(128)S(1)}, s32[16]{0:T(128)}, u32[]{:S(2)}) copy-start(s32[16]{0:T(128)} %param.17) | copy-start | bytes 196
  62.0 31.9 %all-to-all-start.1 = ((bf16[128,2,3584]{2,1,0:T(2,128)(2,1)}), bf16[128,2,3584]{2,1,0:T(2,128)(2,1)S(1)}, u32[]{:S(2)}, u32[]{:S(2)}) async-start(bf16[128,2,3584]{2,1,0:T(2,128)(2,1)} %shard_map.105), calls=%async_computation.1 | async-start | bytes 3670016 | tf_op jit(solution)/shard_map/all_to_all | solution.py:130
  69.6 0.8 copy-start.1

commit v4 on v3

--- a/solution.py
+++ b/solution.py
@@ -32,53 +32,65 @@
     return context.astype(jnp.bfloat16)
 
 
-FF_BLOCK = 256
+FF_BLOCK = 512
 
 
-def expert_kernel(rows_ref, gate_ref, up_ref, down_ref, out_ref, slots_ref, acc_ref):
-    step = pl.program_id(0)
+def expert_kernel(rows_ref, gate_hbm, up_hbm, down_hbm, out_ref,
+                  gate_vmem, up_vmem, down_vmem, slots_ref, acc_ref, sems):
     capacity = rows_ref.shape[1]
-
-    @pl.when(step == 0)
-    def _():
+    blocks = gate_vmem.shape[-1] // FF_BLOCK
+    copies = []
+    for block in range(blocks):
+        cols = pl.ds(block * FF_BLOCK, FF_BLOCK)
+        trio = (
+            pltpu.make_async_copy(gate_hbm.at[0, :, cols], gate_vmem.at[:, cols], sems.at[0, block]),
+            pltpu.make_async_copy(up_hbm.at[0, :, cols], up_vmem.at[:, cols], sems.at[1, block]),
+            pltpu.make_async_copy(down_hbm.at[0, cols, :], down_vmem.at[cols, :], sems.at[2, block]),
+        )
+        for copy in trio:
+            copy.start()
+        copies.append(trio)
+    for slot in range(capacity):
+        slots_ref[slot] = rows_ref[:, slot, :]
+    for block in range(blocks):
+        cols = pl.ds(block * FF_BLOCK, FF_BLOCK)
+        gate_copy, up_copy, down_copy = copies[block]
+        gate_copy.wait()
+        up_copy.wait()
+        down_copy.wait()
         for slot in range(capacity):
-            slots_ref[slot] = rows_ref[:, slot, :]
-        acc_ref[...] = jnp.zeros_like(acc_ref)
-
+            rows = slots_ref[slot]
+            gate_part = jnp.dot(rows, gate_vmem[:, cols], preferred_element_type=jnp.float32)
+            up_part = jnp.dot(rows, up_vmem[:, cols], preferred_element_type=jnp.float32)
+            units = (gate_part / (1.0 + jnp.exp(-gate_part)) * up_part).astype(jnp.bfloat16)
+            partial = jnp.dot(units, down_vmem[cols, :], preferred_element_type=jnp.float32)
+            if block == 0:
+                acc_ref[slot] = partial
+            else:
+                acc_ref[slot] += partial
     for slot in range(capacity):
-        rows = slots_ref[slot]
-        gate_part = jnp.dot(rows, gate_ref[...], preferred_element_type=jnp.float32)
-        up_part = jnp.dot(rows, up_ref[...], preferred_element_type=jnp.float32)
-        units = (gate_part / (1.0 + jnp.exp(-gate_part)) * up_part).astype(jnp.bfloat16)
-        acc_ref[slot] += jnp.dot(units, down_ref[...], preferred_element_type=jnp.float32)
-
-    @pl.when(step == pl.num_programs(0) - 1)
-    def _():
-        for slot in range(capacity):
-            out_ref[:, slot, :] = acc_ref[slot].astype(out_ref.dtype)
+        out_ref[:, slot, :] = acc_ref[slot].astype(out_ref.dtype)
 
 
 def expert_rows(buffer, gate_weight, up_weight, down_weight):
     sources, capacity, model_width = buffer.shape
     hidden_units = gate_weight.shape[-1]
+    in_hbm = pl.BlockSpec(memory_space=pl.ANY)
+    in_vmem = pl.BlockSpec(memory_space=pltpu.VMEM)
     return pl.pallas_call(
         expert_kernel,
-        grid=(hidden_units // FF_BLOCK,),
-        in_specs=[
-            pl.BlockSpec(buffer.shape, lambda f: (0, 0, 0)),
-            pl.BlockSpec((None, model_width, FF_BLOCK), lambda f: (0, 0, f)),
-            pl.BlockSpec((None, model_width, FF_BLOCK), lambda f: (0, 0, f)),
-            pl.BlockSpec((None, FF_BLOCK, model_width), lambda f: (0, f, 0)),
-        ],
-        out_specs=pl.BlockSpec(buffer.shape, lambda f: (0, 0, 0)),
+        in_specs=[in_vmem, in_hbm, in_hbm, in_hbm],
+        out_specs=in_vmem,
         out_shape=jax.ShapeDtypeStruct(buffer.shape, jnp.bfloat16),
         scratch_shapes=[
+            pltpu.VMEM((model_width, hidden_units), jnp.bfloat16),
+            pltpu.VMEM((model_width, hidden_units), jnp.bfloat16),
+            pltpu.VMEM((hidden_units, model_width), jnp.bfloat16),
             pltpu.VMEM((capacity, sources, model_width), jnp.bfloat16),
             pltpu.VMEM((capacity, sources, model_width), jnp.float32),
+            pltpu.SemaphoreType.DMA((3, hidden_units // FF_BLOCK)),
         ],
-        compiler_params=pltpu.CompilerParams(
-            dimension_semantics=("arbitrary",), vmem_limit_bytes=48 * 1024 * 1024
-        ),
+        compiler_params=pltpu.CompilerParams(vmem_limit_bytes=56 * 1024 * 1024),
     )(buffer, gate_weight, up_weight, down_weight)
 
 

time: 95.7 us -> 92.1 us (0.962)
  Pallas kernels: 20.5 us -> 16.9 us
    pallas_call x1, Pallas kernels: 17.5 us -> 13.8 us  [expert_rows(): pl.pallas_call(expert_kernel, in_specs=[in_vmem, in_hbm, in_hbm, in_hbm],...]
  transfers between devices with their start and end apart: 1 -> 1, of which waited for: 1 -> 1; matrix products, arithmetic and copies ran while one was open for 8% -> 9% of each run, Pallas kernels for 0% -> 0%
where the time goes in v4:
time: 92.1 us; the launch traced here: 91.8 us
  blocking collectives  38.4 us (42%)
  waiting for transfers between devices  18.3 us (20%)
  Pallas kernels  16.9 us (18%)
  matrix products  8.61 us (9%)
  starting transfers between devices  4.84 us (5%)
  local copies, waits for them, and re-layouts  2.67 us (3%)
  other arithmetic  1.26 us (1%)
    all_to_all x1, blocking collectives, shards(): lax.all_to_all(outgoing, ('row', 'col'), split_axis=0, concat_axis=0, til...  38.4 us
    all_to_all x1, waiting for transfers between devices, shards(): lax.all_to_all(computed, ('row', 'col'), split_axis=0, concat_axis=0, til...  18.3 us
    pallas_call x1, Pallas kernels, expert_rows(): pl.pallas_call(expert_kernel, in_specs=[in_vmem, in_hbm, in_hbm, in_hbm],...  13.8 us
    all_to_all x1, starting transfers between devices, shards(): lax.all_to_all(computed, ('row', 'col'), split_axis=0, concat_axis=0, til...  4.84 us
    dot_general x1, matrix products, attention(): jnp.einsum('shl,slc->shc', probabilities, latent_cache[:, :, :LATENT], pr...  4.82 us
    pallas_call x1, Pallas kernels, shards(): pl.pallas_call(dispatch_kernel, out_shape=jax.ShapeDtypeStruct((experts,...  3.07 us
    dot_general x1, matrix products, attention(): jnp.einsum('shc,slc->shl', queries, latent_cache, preferred_element_type=...  2.32 us
  transfers between devices with their start and end apart: 1, of which 1 were waited for; matrix products, arithmetic and copies ran while one was open for 9% of the time, Pallas kernels for 0%

profile of v4, /device:TPU:0, one launch (start us, length us, event | category | flops | bytes accessed | tf_op | source)
XLA Modules:
  0.0 91.8 jit_solution(12242384720837806481)
XLA Ops:
  0.6 0.0 copy-start
  0.6 0.9 copy.21
  1.5 0.1 eq.48
  1.6 0.1 convert_compare_fusion
  1.7 0.1 fusion.14
  1.8 0.2 reduce_window_sum.11
  2.0 0.2 select_reduce_fusion
  2.1 0.1 eq.52
  2.2 0.1 and_reduce_fusion
  2.4 0.7 copy.24
  3.1 3.1 %shard_map.104 = bf16[128,2,3584]{2,1,0:T(2,128)(2,1)} custom-call(bf16[2,128,16]{2,1,0:T(8,128)(2,1)} %bitcast.12, bf16[16,3584]{1,0:T(8,128)(2,1)} %hidden_ref.1), custom_call_target="tpu_custom_call" | custom-call | tf_op jit(solution)/shard_map/pallas_call | solution.py:132
  6.2 38.4 %all_to_all.10.rows_ref = bf16[128,2,3584]{2,1,0:T(2,128)(2,1)} all-to-all(bf16[128,2,3584]{2,1,0:T(2,128)(2,1)} %shard_map.104), channel_id=1, replica_groups=mesh['row'=8,'col'=16] {'row','col'}, dimensions={0} | all-to-all | bytes 3670016 | tf_op jit(solution)/shard_map/all_to_all | solution.py:137
  44.6 13.8 %shard_map.105 = bf16[128,2,3584]{2,1,0:T(2,128)(2,1)} custom-call(bf16[128,2,3584]{2,1,0:T(2,128)(2,1)} %all_to_all.10.rows_ref, bf16[1,3584,1024]{2,1,0:T(8,128)(2,1)} %gate_hbm.1, bf16[1,3584,1024]{2,1,0:T(8,128)(2,1)} %up_hbm.1, bf16[1,1024,3584]{2,1,0:T(8,128)(2,1)} %down_hbm.1), custom_call_target="tpu_custom_call" | custom-call | tf_op jit(solution)/shard_map/pallas_call | solution.py:80
  58.4 0.0 copy-start.2
  58.5 0.0 copy-start.3
  58.5 4.8 %all-to-all-start.1 = ((bf16[128,2,3584]{2,1,0:T(2,128)(2,1)}), bf16[128,2,3584]{2,1,0:T(2,128)(2,1)S(1)}, u32[]{:S(2)}, u32[]{:S(2)}) async-start(bf16[128,2,3584]{2,1,0:T(2,128)(2,1)} %shard_map.105), calls=%async_computation.1 | async-start | bytes 3670016 | tf_op jit(solution)/shard_map/all_to_all | solution.py:142
  63.3 0.0 copy-done.2
  63.4 0.1 copy.23
  63.4 0.1 fusion.13
  63.6 0.0 copy-done.3
  63.6 0.1 iota_compare_fusion.3
  63.7 0.0 copy-done
  63.7 2.3 %fusion.11 = f32[16,64,128]{2,1,0:T(8,128)S(1)} fusion(bf16[16,64,576]{2,1,0:T(8,128)(2,1)S(1)} %copy-done, bf16[16,128,576]{1,2,0:T(8,128)(2,1)} %param.16, pred[16,128]{1,0:T(8,128)(4,1)S(1)} %iota_compare_fusion.3), kind=kOutput, calls=%fused_computation.11 | convolution fusion | flops 151257088 | bytes 4065280 | tf_op jit(solution)/shard_map/shc,slc->shl/dot_general | solution.py:16
  66.0 0.0 copy-start.1
  66.0 0.8 copy-done.1
  66.8 0.3 fusion.18
  67.2 4.8 %fusion.5 = bf16[16,64,512]{2,1,0:T(8,128)(2,1)} fusion(bf16[16,128,576]{1,2,0:T(8,128)(2,1)} %param.16, f32[16,64]{1,0:T(8,128)S(1)} %fusion.18, f32[16,64,128]{2,1,0:T(8,128)} %copy-done.1, pred[16,128]{1,0:T(8,128)(4,1)S(1)} %iota_compare_fusion.3), kind=kOutput, calls=%fused_computation.6 | convolution fusion | flops 135267456 | bytes 4200448 | tf_op jit(solution)/shard_map/shl,slc->shc/dot_general | solution.py:26
  72.0 18.3 %all-to-all-done.1 = bf16[128,2,3584]{2,1,0:T(2,128)(2,1)S(1)} async-done(((bf16[128,2,3584]{2,1,0:T(2,128)(2,1)}), bf16[128,2,3584]{2,1,0:T(2,128)(2,1)S(1)}, u32[]{:S(2)}, u32[]{:S(2)}) %all-to-all-start.1) | async-done | bytes 1835040 | tf_op jit(solution)/shard_map/all_to_all | solution.py:142
  90.3 1.5 %fusion.1 = bf16[16,3584]{1,0:T(8,128)(2,1)} fusion(bf16[128,2,3584]{2,1,0:T(2,128)(2,1)S(1)} %all-to-all-done.1, f32[2,16,128]{2,1,0:T(8,128)S(1)} %fusion.13), kind=kOutput, calls=%fused_computation.2 | convolution fusion | flops 176218112 | bytes 1966080 | tf_op jit(solution)/shard_map/dot_general | solution.py:145
  (4 shorter events, 0.1 us)
Async XLA Ops:
  0.6 63.0 %copy-start = (bf16[16,64,576]{2,1,0:T(8,128)(2,1)S(1)}, bf16[16,64,576]{2,1,0:T(8,128)(2,1)}, u32[]{:S(2)}) copy-start(bf16[16,64,576]{2,1,0:T(8,128)(2,1)} %param.15) | copy-start | bytes 3538948
  58.4 4.9 %copy-start.2 = (f32[16,8]{0,1:T(8,128)S(1)}, f32[16,8]{0,1:T(8,128)}, u32[]{:S(2)}) copy-start(f32[16,8]{0,1:T(8,128)} %param.11) | copy-start | bytes 1540
  58.5 5.1 %copy-start.3 = (s32[16]{0:T(128)S(1)}, s32[16]{0:T(128)}, u32[]{:S(2)}) copy-start(s32[16]{0:T(128)} %param.17) | copy-start | bytes 196
  58.5 31.8 %all-to-all-start.1 = ((bf16[128,2,3584]{2,1,0:T(2,128)(2,1)}), bf16[128,2,3584]{2,1,0:T(2,128)(2,1)S(1)}, u32[]{:S(2)}, u32[]{:S(2)}) async-start(bf16[128,2,3584]{2,1,0:T(2,128)(2,1)} %shard_map.105), calls=%async_computation.1 | async-start | bytes 3670016 | tf_op jit(solution)/shard_map/all_to_all | solution.py:142
  66.0 0.8 copy-start.1

commit v5 on v4

--- a/solution.py
+++ b/solution.py
@@ -133,12 +133,10 @@
         dispatch_kernel,
         out_shape=jax.ShapeDtypeStruct((experts, capacity, model_width), jnp.bfloat16),
     )(layout, hidden)
-    computed = expert_rows(
-        lax.all_to_all(outgoing, ("row", "col"), split_axis=0, concat_axis=0, tiled=True),
-        gate_weight,
-        up_weight,
-        down_weight,
-    )
+    context = attention(queries, latent_cache, lengths)
+    received = lax.all_to_all(outgoing, ("row", "col"), split_axis=0, concat_axis=0, tiled=True)
+    context, received = lax.optimization_barrier((context, received))
+    computed = expert_rows(received, gate_weight, up_weight, down_weight)
     returned = lax.all_to_all(computed, ("row", "col"), split_axis=0, concat_axis=0, tiled=True)
     mixing = jnp.transpose(mixing, (1, 2, 0)).reshape(seq_dev, experts * capacity)
     returned = returned.reshape(experts * capacity, model_width)
@@ -148,7 +146,6 @@
         precision=lax.Precision.HIGHEST,
         preferred_element_type=jnp.float32,
     ).astype(jnp.bfloat16)
-    context = attention(queries, latent_cache, lengths)
     return (mixture, context)
 
 

time: 92.1 us -> 93.3 us (1.013)
  blocking collectives: 38.4 us -> 0 us
  waiting for transfers between devices: 18.3 us -> 45.6 us
  starting transfers between devices: 4.84 us -> 15.8 us
  local copies, waits for them, and re-layouts: 2.67 us -> 3.92 us
    all_to_all x1 -> x0, blocking collectives: 38.4 us -> none  [shards(): lax.all_to_all(outgoing, ('row', 'col'), split_axis=0, concat_axis=0, til...]
    all_to_all x0 -> x1, waiting for transfers between devices: none -> 18.7 us  [shards(): lax.all_to_all(outgoing, ('row', 'col'), split_axis=0, concat_axis=0, til...]
    all_to_all x0 -> x1, starting transfers between devices: none -> 11.2 us  [shards(): lax.all_to_all(outgoing, ('row', 'col'), split_axis=0, concat_axis=0, til...]
    all_to_all x1, waiting for transfers between devices: 18.3 us -> 26.9 us  [shards(): lax.all_to_all(computed, ('row', 'col'), split_axis=0, concat_axis=0, til...]
    unnamed x9 -> x11, local copies, waits for them, and re-layouts: 1.69 us -> 2.94 us
  transfers between devices with their start and end apart: 1 -> 2, of which waited for: 1 -> 2; matrix products, arithmetic and copies ran while one was open for 9% -> 8% of each run, Pallas kernels for 0% -> 0%
where the time goes in v5:
time: 93.3 us; the launch traced here: 92.9 us
  waiting for transfers between devices  45.6 us (49%)
  Pallas kernels  16.9 us (18%)
  starting transfers between devices  15.8 us (17%)
  matrix products  8.62 us (9%)
  local copies, waits for them, and re-layouts  3.92 us (4%)
  other arithmetic  1.26 us (1%)
    all_to_all x1, waiting for transfers between devices, shards(): lax.all_to_all(computed, ('row', 'col'), split_axis=0, concat_axis=0, til...  26.9 us
    all_to_all x1, waiting for transfers between devices, shards(): lax.all_to_all(outgoing, ('row', 'col'), split_axis=0, concat_axis=0, til...  18.7 us
    pallas_call x1, Pallas kernels, expert_rows(): pl.pallas_call(expert_kernel, in_specs=[in_vmem, in_hbm, in_hbm, in_hbm],...  13.8 us
    all_to_all x1, starting transfers between devices, shards(): lax.all_to_all(outgoing, ('row', 'col'), split_axis=0, concat_axis=0, til...  11.2 us
    dot_general x1, matrix products, attention(): jnp.einsum('shl,slc->shc', probabilities, latent_cache[:, :, :LATENT], pr...  4.82 us
    all_to_all x1, starting transfers between devices, shards(): lax.all_to_all(computed, ('row', 'col'), split_axis=0, concat_axis=0, til...  4.66 us
    pallas_call x1, Pallas kernels, shards(): pl.pallas_call(dispatch_kernel, out_shape=jax.ShapeDtypeStruct((experts,...  3.06 us
    unnamed x11, local copies, waits for them, and re-layouts  2.94 us
  transfers between devices with their start and end apart: 2, of which 2 were waited for; matrix products, arithmetic and copies ran while one was open for 8% of the time, Pallas kernels for 0%

profile of v5, /device:TPU:0, one launch (start us, length us, event | category | flops | bytes accessed | tf_op | source)
XLA Modules:
  0.0 92.9 jit_solution(1969869674676750071)
XLA Ops:
  0.6 0.0 copy-start
  0.6 0.9 copy.21
  1.5 0.1 eq.48
  1.6 0.1 convert_compare_fusion
  1.7 0.1 fusion.14
  1.8 0.2 reduce_window_sum.11
  2.0 0.2 select_reduce_fusion
  2.1 0.1 eq.52
  2.2 0.1 and_reduce_fusion
  2.4 0.7 copy.25
  3.1 3.1 %shard_map.104 = bf16[128,2,3584]{2,1,0:T(2,128)(2,1)} custom-call(bf16[2,128,16]{2,1,0:T(8,128)(2,1)} %bitcast.12, bf16[16,3584]{1,0:T(8,128)(2,1)} %hidden_ref.1), custom_call_target="tpu_custom_call" | custom-call | tf_op jit(solution)/shard_map/pallas_call | solution.py:132
  6.2 0.0 copy-start.4
  6.2 11.2 %all-to-all-start = ((bf16[128,2,3584]{2,1,0:T(2,128)(2,1)}), bf16[128,2,3584]{2,1,0:T(2,128)(2,1)S(1)}, u32[]{:S(2)}, u32[]{:S(2)}) async-start(bf16[128,2,3584]{2,1,0:T(2,128)(2,1)} %shard_map.104), calls=%async_computation | async-start | bytes 3670016 | tf_op jit(solution)/shard_map/all_to_all | solution.py:137
  17.4 0.0 copy-done.4
  17.4 0.1 iota_compare_fusion.3
  17.4 0.0 copy-done
  17.5 2.3 %fusion.11 = f32[16,64,128]{2,1,0:T(8,128)S(1)} fusion(bf16[16,64,576]{2,1,0:T(8,128)(2,1)S(1)} %copy-done, bf16[16,128,576]{1,2,0:T(8,128)(2,1)} %param.16, pred[16,128]{1,0:T(8,128)(4,1)S(1)} %iota_compare_fusion.3), kind=kOutput, calls=%fused_computation.11 | convolution fusion | flops 151257088 | bytes 4065280 | tf_op jit(solution)/shard_map/shc,slc->shl/dot_general | solution.py:16
  19.8 0.0 copy-start.2
  19.8 0.8 copy-done.2
  20.6 0.3 fusion.18
  20.9 4.8 %fusion.5 = bf16[16,64,512]{2,1,0:T(8,128)(2,1)} fusion(bf16[16,128,576]{1,2,0:T(8,128)(2,1)} %param.16, f32[16,64]{1,0:T(8,128)S(1)} %fusion.18, f32[16,64,128]{2,1,0:T(8,128)} %copy-done.2, pred[16,128]{1,0:T(8,128)(4,1)S(1)} %iota_compare_fusion.3), kind=kOutput, calls=%fused_computation.6 | convolution fusion | flops 135267456 | bytes 4200448 | tf_op jit(solution)/shard_map/shl,slc->shc/dot_general | solution.py:26
  25.8 18.7 %all-to-all-done.rows_ref = bf16[128,2,3584]{2,1,0:T(2,128)(2,1)S(1)} async-done(((bf16[128,2,3584]{2,1,0:T(2,128)(2,1)}), bf16[128,2,3584]{2,1,0:T(2,128)(2,1)S(1)}, u32[]{:S(2)}, u32[]{:S(2)}) %all-to-all-start) | async-done | bytes 1835040 | tf_op jit(solution)/shard_map/all_to_all | solution.py:137
  44.5 0.0 copy-start.1
  44.5 1.3 %copy-done.1 = bf16[128,2,3584]{2,1,0:T(2,128)(2,1)} copy-done((bf16[128,2,3584]{2,1,0:T(2,128)(2,1)}, bf16[128,2,3584]{2,1,0:T(2,128)(2,1)S(1)}, u32[]{:S(2)}) %copy-start.1) | copy-done | bytes 1835032
  45.8 13.8 %shard_map.105 = bf16[128,2,3584]{2,1,0:T(2,128)(2,1)} custom-call(bf16[128,2,3584]{2,1,0:T(2,128)(2,1)} %copy-done.1, bf16[1,3584,1024]{2,1,0:T(8,128)(2,1)} %gate_hbm.1, bf16[1,3584,1024]{2,1,0:T(8,128)(2,1)} %up_hbm.1, bf16[1,1024,3584]{2,1,0:T(8,128)(2,1)} %down_hbm.1), custom_call_target="tpu_custom_call" | custom-call | tf_op jit(solution)/shard_map/pallas_call | solution.py:80
  59.6 0.0 copy-start.3
  59.6 4.7 %all-to-all-start.1 = ((bf16[128,2,3584]{2,1,0:T(2,128)(2,1)}), bf16[128,2,3584]{2,1,0:T(2,128)(2,1)S(1)}, u32[]{:S(2)}, u32[]{:S(2)}) async-start(bf16[128,2,3584]{2,1,0:T(2,128)(2,1)} %shard_map.105), calls=%async_computation.1 | async-start | bytes 3670016 | tf_op jit(solution)/shard_map/all_to_all | solution.py:140
  64.3 0.0 copy-done.3
  64.3 0.1 copy.23
  64.4 0.1 fusion.13
  64.5 26.9 %all-to-all-done.1 = bf16[128,2,3584]{2,1,0:T(2,128)(2,1)S(1)} async-done(((bf16[128,2,3584]{2,1,0:T(2,128)(2,1)}), bf16[128,2,3584]{2,1,0:T(2,128)(2,1)S(1)}, u32[]{:S(2)}, u32[]{:S(2)}) %all-to-all-start.1) | async-done | bytes 1835040 | tf_op jit(solution)/shard_map/all_to_all | solution.py:140
  91.4 1.5 %fusion.1 = bf16[16,3584]{1,0:T(8,128)(2,1)} fusion(bf16[128,2,3584]{2,1,0:T(2,128)(2,1)S(1)} %all-to-all-done.1, f32[2,16,128]{2,1,0:T(8,128)S(1)} %fusion.13), kind=kOutput, calls=%fused_computation.2 | convolution fusion | flops 176218112 | bytes 1966080 | tf_op jit(solution)/shard_map/dot_general | solution.py:143
  (4 shorter events, 0.1 us)
Async XLA Ops:
  0.6 16.8 %copy-start = (bf16[16,64,576]{2,1,0:T(8,128)(2,1)S(1)}, bf16[16,64,576]{2,1,0:T(8,128)(2,1)}, u32[]{:S(2)}) copy-start(bf16[16,64,576]{2,1,0:T(8,128)(2,1)} %param.15) | copy-start | bytes 3538948
  6.2 11.2 %copy-start.4 = (s32[16]{0:T(128)S(1)}, s32[16]{0:T(128)}, u32[]{:S(2)}) copy-start(s32[16]{0:T(128)} %param.17) | copy-start | bytes 196
  6.2 38.3 %all-to-all-start = ((bf16[128,2,3584]{2,1,0:T(2,128)(2,1)}), bf16[128,2,3584]{2,1,0:T(2,128)(2,1)S(1)}, u32[]{:S(2)}, u32[]{:S(2)}) async-start(bf16[128,2,3584]{2,1,0:T(2,128)(2,1)} %shard_map.104), calls=%async_computation | async-start | bytes 3670016 | tf_op jit(solution)/shard_map/all_to_all | solution.py:137
  19.8 0.8 copy-start.2
  44.5 1.3 %copy-start.1 = (bf16[128,2,3584]{2,1,0:T(2,128)(2,1)}, bf16[128,2,3584]{2,1,0:T(2,128)(2,1)S(1)}, u32[]{:S(2)}) copy-start(bf16[128,2,3584]{2,1,0:T(2,128)(2,1)S(1)} %all-to-all-done.rows_ref) | copy-start | bytes 5505028
  59.6 4.7 %copy-start.3 = (f32[16,8]{0,1:T(8,128)S(1)}, f32[16,8]{0,1:T(8,128)}, u32[]{:S(2)}) copy-start(f32[16,8]{0,1:T(8,128)} %param.11) | copy-start | bytes 1540
  59.6 31.8 %all-to-all-start.1 = ((bf16[128,2,3584]{2,1,0:T(2,128)(2,1)}), bf16[128,2,3584]{2,1,0:T(2,128)(2,1)S(1)}, u32[]{:S(2)}, u32[]{:S(2)}) async-start(bf16[128,2,3584]{2,1,0:T(2,128)(2,1)} %shard_map.105), calls=%async_computation.1 | async-start | bytes 3670016 | tf_op jit(solution)/shard_map/all_to_all | solution.py:140

commit v6 on v4

--- a/solution.py
+++ b/solution.py
@@ -32,32 +32,37 @@
     return context.astype(jnp.bfloat16)
 
 
-FF_BLOCK = 512
+FF_BLOCKS = (512, 512)
+LOOKAHEAD = 1
 
 
 def expert_kernel(rows_ref, gate_hbm, up_hbm, down_hbm, out_ref,
                   gate_vmem, up_vmem, down_vmem, slots_ref, acc_ref, sems):
     capacity = rows_ref.shape[1]
-    blocks = gate_vmem.shape[-1] // FF_BLOCK
+    bounds = [0]
+    for width in FF_BLOCKS:
+        bounds.append(bounds[-1] + width)
+    spans = [pl.ds(low, high - low) for low, high in zip(bounds[:-1], bounds[1:])]
     copies = []
-    for block in range(blocks):
-        cols = pl.ds(block * FF_BLOCK, FF_BLOCK)
-        trio = (
+    for block, cols in enumerate(spans):
+        copies.append((
             pltpu.make_async_copy(gate_hbm.at[0, :, cols], gate_vmem.at[:, cols], sems.at[0, block]),
             pltpu.make_async_copy(up_hbm.at[0, :, cols], up_vmem.at[:, cols], sems.at[1, block]),
             pltpu.make_async_copy(down_hbm.at[0, cols, :], down_vmem.at[cols, :], sems.at[2, block]),
-        )
-        for copy in trio:
+        ))
+    for block in range(min(LOOKAHEAD, len(spans))):
+        for copy in copies[block]:
             copy.start()
-        copies.append(trio)
     for slot in range(capacity):
         slots_ref[slot] = rows_ref[:, slot, :]
-    for block in range(blocks):
-        cols = pl.ds(block * FF_BLOCK, FF_BLOCK)
+    for block, cols in enumerate(spans):
         gate_copy, up_copy, down_copy = copies[block]
         gate_copy.wait()
         up_copy.wait()
         down_copy.wait()
+        if block + LOOKAHEAD < len(spans):
+            for copy in copies[block + LOOKAHEAD]:
+                copy.start()
         for slot in range(capacity):
             rows = slots_ref[slot]
             gate_part = jnp.dot(rows, gate_vmem[:, cols], preferred_element_type=jnp.float32)
@@ -88,7 +93,7 @@
             pltpu.VMEM((hidden_units, model_width), jnp.bfloat16),
             pltpu.VMEM((capacity, sources, model_width), jnp.bfloat16),
             pltpu.VMEM((capacity, sources, model_width), jnp.float32),
-            pltpu.SemaphoreType.DMA((3, hidden_units // FF_BLOCK)),
+            pltpu.SemaphoreType.DMA((3, len(FF_BLOCKS))),
         ],
         compiler_params=pltpu.CompilerParams(vmem_limit_bytes=56 * 1024 * 1024),
     )(buffer, gate_weight, up_weight, down_weight)
@@ -97,7 +102,10 @@
 def dispatch_kernel(layout_ref, hidden_ref, out_ref):
     hidden_rows = hidden_ref[...]
     for slot in range(out_ref.shape[1]):
-        placed = jnp.dot(layout_ref[slot], hidden_rows, preferred_element_type=jnp.float32)
+        placed = lax.dot_general(
+            layout_ref[slot], hidden_rows, (((0,), (0,)), ((), ())),
+            preferred_element_type=jnp.float32,
+        )
         out_ref[:, slot, :] = placed.astype(out_ref.dtype)
 
 
@@ -127,7 +135,7 @@
         (onehot[None, :, :] > 0)
         & (ranking[None, :, None] == jnp.arange(capacity, dtype=jnp.int32)[:, None, None])
     ).reshape(capacity, seq_dev, top_count, experts)
-    layout = jnp.swapaxes(jnp.any(share, axis=2), 1, 2).astype(jnp.bfloat16)
+    layout = jnp.any(share, axis=2).astype(jnp.bfloat16)
     mixing = jnp.sum(share.astype(jnp.float32) * combine[None, :, :, None], axis=2)
     outgoing = pl.pallas_call(
         dispatch_kernel,

time: 92.1 us -> 93.1 us (1.011)
  Pallas kernels: 16.9 us -> 17.9 us
    pallas_call x1, Pallas kernels: 13.8 us -> 14.8 us  [expert_rows(): pl.pallas_call(expert_kernel, in_specs=[in_vmem, in_hbm, in_hbm, in_hbm],...]
  transfers between devices with their start and end apart: 1 -> 1, of which waited for: 1 -> 1; matrix products, arithmetic and copies ran while one was open for 9% -> 8% of each run, Pallas kernels for 0% -> 0%
where the time goes in v6:
time: 93.1 us; the launch traced here: 92.6 us
  blocking collectives  38.4 us (41%)
  waiting for transfers between devices  18.3 us (20%)
  Pallas kernels  17.9 us (19%)
  matrix products  8.61 us (9%)
  starting transfers between devices  4.84 us (5%)
  local copies, waits for them, and re-layouts  1.93 us (2%)
  other arithmetic  1.86 us (2%)
    all_to_all x1, blocking collectives, shards(): lax.all_to_all(outgoing, ('row', 'col'), split_axis=0, concat_axis=0, til...  38.4 us
    all_to_all x1, waiting for transfers between devices, shards(): lax.all_to_all(computed, ('row', 'col'), split_axis=0, concat_axis=0, til...  18.3 us
    pallas_call x1, Pallas kernels, expert_rows(): pl.pallas_call(expert_kernel, in_specs=[in_vmem, in_hbm, in_hbm, in_hbm],...  14.8 us
    all_to_all x1, starting transfers between devices, shards(): lax.all_to_all(computed, ('row', 'col'), split_axis=0, concat_axis=0, til...  4.84 us
    dot_general x1, matrix products, attention(): jnp.einsum('shl,slc->shc', probabilities, latent_cache[:, :, :LATENT], pr...  4.82 us
    pallas_call x1, Pallas kernels, shards(): pl.pallas_call(dispatch_kernel, out_shape=jax.ShapeDtypeStruct((experts,...  3.1 us
    dot_general x1, matrix products, attention(): jnp.einsum('shc,slc->shl', queries, latent_cache, preferred_element_type=...  2.32 us
  transfers between devices with their start and end apart: 1, of which 1 were waited for; matrix products, arithmetic and copies ran while one was open for 8% of the time, Pallas kernels for 0%

profile of v6, /device:TPU:0, one launch (start us, length us, event | category | flops | bytes accessed | tf_op | source)
XLA Modules:
  0.0 92.6 jit_solution(7824261574315940018)
XLA Ops:
  0.6 0.0 copy-start
  0.6 0.9 copy.21
  1.5 0.1 eq.48
  1.6 0.1 convert_compare_fusion
  1.7 0.1 fusion.14
  1.8 0.2 reduce_window_sum.11
  2.0 0.2 select_reduce_fusion
  2.1 0.1 eq.52
  2.2 0.1 and_reduce_fusion
  2.4 0.6 convert_element_type.25.layout_ref
  3.0 3.1 %shard_map.104 = bf16[128,2,3584]{2,1,0:T(2,128)(2,1)} custom-call(bf16[2,16,128]{2,1,0:T(8,128)(2,1)} %convert_element_type.25.layout_ref, bf16[16,3584]{1,0:T(8,128)(2,1)} %hidden_ref.1), custom_call_target="tpu_custom_call" | custom-call | tf_op jit(solution)/shard_map/pallas_call | solution.py:140
  6.1 38.4 %all_to_all.10.rows_ref = bf16[128,2,3584]{2,1,0:T(2,128)(2,1)} all-to-all(bf16[128,2,3584]{2,1,0:T(2,128)(2,1)} %shard_map.104), channel_id=1, replica_groups=mesh['row'=8,'col'=16] {'row','col'}, dimensions={0} | all-to-all | bytes 3670016 | tf_op jit(solution)/shard_map/all_to_all | solution.py:145
  44.5 14.8 %shard_map.105 = bf16[128,2,3584]{2,1,0:T(2,128)(2,1)} custom-call(bf16[128,2,3584]{2,1,0:T(2,128)(2,1)} %all_to_all.10.rows_ref, bf16[1,3584,1024]{2,1,0:T(8,128)(2,1)} %gate_hbm.1, bf16[1,3584,1024]{2,1,0:T(8,128)(2,1)} %up_hbm.1, bf16[1,1024,3584]{2,1,0:T(8,128)(2,1)} %down_hbm.1), custom_call_target="tpu_custom_call" | custom-call | tf_op jit(solution)/shard_map/pallas_call | solution.py:85
  59.3 0.0 copy-start.2
  59.3 0.0 copy-start.3
  59.4 4.8 %all-to-all-start.1 = ((bf16[128,2,3584]{2,1,0:T(2,128)(2,1)}), bf16[128,2,3584]{2,1,0:T(2,128)(2,1)S(1)}, u32[]{:S(2)}, u32[]{:S(2)}) async-start(bf16[128,2,3584]{2,1,0:T(2,128)(2,1)} %shard_map.105), calls=%async_computation.1 | async-start | bytes 3670016 | tf_op jit(solution)/shard_map/all_to_all | solution.py:150
  64.2 0.0 copy-done.2
  64.2 0.1 copy.23
  64.3 0.1 fusion.13
  64.5 0.0 copy-done.3
  64.5 0.1 iota_compare_fusion.3
  64.6 0.0 copy-done
  64.6 2.3 %fusion.11 = f32[16,64,128]{2,1,0:T(8,128)S(1)} fusion(bf16[16,64,576]{2,1,0:T(8,128)(2,1)S(1)} %copy-done, bf16[16,128,576]{1,2,0:T(8,128)(2,1)} %param.16, pred[16,128]{1,0:T(8,128)(4,1)S(1)} %iota_compare_fusion.3), kind=kOutput, calls=%fused_computation.11 | convolution fusion | flops 151257088 | bytes 4065280 | tf_op jit(solution)/shard_map/shc,slc->shl/dot_general | solution.py:16
  66.9 0.0 copy-start.1
  66.9 0.8 copy-done.1
  67.7 0.3 fusion.18
  68.0 4.8 %fusion.5 = bf16[16,64,512]{2,1,0:T(8,128)(2,1)} fusion(bf16[16,128,576]{1,2,0:T(8,128)(2,1)} %param.16, f32[16,64]{1,0:T(8,128)S(1)} %fusion.18, f32[16,64,128]{2,1,0:T(8,128)} %copy-done.1, pred[16,128]{1,0:T(8,128)(4,1)S(1)} %iota_compare_fusion.3), kind=kOutput, calls=%fused_computation.6 | convolution fusion | flops 135267456 | bytes 4200448 | tf_op jit(solution)/shard_map/shl,slc->shc/dot_general | solution.py:26
  72.9 18.3 %all-to-all-done.1 = bf16[128,2,3584]{2,1,0:T(2,128)(2,1)S(1)} async-done(((bf16[128,2,3584]{2,1,0:T(2,128)(2,1)}), bf16[128,2,3584]{2,1,0:T(2,128)(2,1)S(1)}, u32[]{:S(2)}, u32[]{:S(2)}) %all-to-all-start.1) | async-done | bytes 1835040 | tf_op jit(solution)/shard_map/all_to_all | solution.py:150
  91.2 1.5 %fusion.1 = bf16[16,3584]{1,0:T(8,128)(2,1)} fusion(bf16[128,2,3584]{2,1,0:T(2,128)(2,1)S(1)} %all-to-all-done.1, f32[2,16,128]{2,1,0:T(8,128)S(1)} %fusion.13), kind=kOutput, calls=%fused_computation.2 | convolution fusion | flops 176218112 | bytes 1966080 | tf_op jit(solution)/shard_map/dot_general | solution.py:153
  (3 shorter events, 0.0 us)
Async XLA Ops:
  0.6 63.9 %copy-start = (bf16[16,64,576]{2,1,0:T(8,128)(2,1)S(1)}, bf16[16,64,576]{2,1,0:T(8,128)(2,1)}, u32[]{:S(2)}) copy-start(bf16[16,64,576]{2,1,0:T(8,128)(2,1)} %param.15) | copy-start | bytes 3538948
  59.3 4.9 %copy-start.2 = (f32[16,8]{0,1:T(8,128)S(1)}, f32[16,8]{0,1:T(8,128)}, u32[]{:S(2)}) copy-start(f32[16,8]{0,1:T(8,128)} %param.11) | copy-start | bytes 1540
  59.3 5.1 %copy-start.3 = (s32[16]{0:T(128)S(1)}, s32[16]{0:T(128)}, u32[]{:S(2)}) copy-start(s32[16]{0:T(128)} %param.17) | copy-start | bytes 196
  59.4 31.8 %all-to-all-start.1 = ((bf16[128,2,3584]{2,1,0:T(2,128)(2,1)}), bf16[128,2,3584]{2,1,0:T(2,128)(2,1)S(1)}, u32[]{:S(2)}, u32[]{:S(2)}) async-start(bf16[128,2,3584]{2,1,0:T(2,128)(2,1)} %shard_map.105), calls=%async_computation.1 | async-start | bytes 3670016 | tf_op jit(solution)/shard_map/all_to_all | solution.py:150
  66.9 0.8 copy-start.1

commit v7 on v4

--- a/solution.py
+++ b/solution.py
@@ -97,7 +97,10 @@
 def dispatch_kernel(layout_ref, hidden_ref, out_ref):
     hidden_rows = hidden_ref[...]
     for slot in range(out_ref.shape[1]):
-        placed = jnp.dot(layout_ref[slot], hidden_rows, preferred_element_type=jnp.float32)
+        placed = lax.dot_general(
+            layout_ref[slot], hidden_rows, (((0,), (0,)), ((), ())),
+            preferred_element_type=jnp.float32,
+        )
         out_ref[:, slot, :] = placed.astype(out_ref.dtype)
 
 
@@ -127,7 +130,7 @@
         (onehot[None, :, :] > 0)
         & (ranking[None, :, None] == jnp.arange(capacity, dtype=jnp.int32)[:, None, None])
     ).reshape(capacity, seq_dev, top_count, experts)
-    layout = jnp.swapaxes(jnp.any(share, axis=2), 1, 2).astype(jnp.bfloat16)
+    layout = jnp.any(share, axis=2).astype(jnp.bfloat16)
     mixing = jnp.sum(share.astype(jnp.float32) * combine[None, :, :, None], axis=2)
     outgoing = pl.pallas_call(
         dispatch_kernel,

time: 92.1 us -> 92.1 us (level)
  no operation moved by 1% of the time
where the time goes in v7:
time: 92.1 us; the launch traced here: 91.6 us
  blocking collectives  38.4 us (42%)
  waiting for transfers between devices  18.3 us (20%)
  Pallas kernels  16.9 us (18%)
  matrix products  8.61 us (9%)
  starting transfers between devices  4.84 us (5%)
  local copies, waits for them, and re-layouts  1.93 us (2%)
  other arithmetic  1.86 us (2%)
    all_to_all x1, blocking collectives, shards(): lax.all_to_all(outgoing, ('row', 'col'), split_axis=0, concat_axis=0, til...  38.4 us
    all_to_all x1, waiting for transfers between devices, shards(): lax.all_to_all(computed, ('row', 'col'), split_axis=0, concat_axis=0, til...  18.3 us
    pallas_call x1, Pallas kernels, expert_rows(): pl.pallas_call(expert_kernel, in_specs=[in_vmem, in_hbm, in_hbm, in_hbm],...  13.8 us
    all_to_all x1, starting transfers between devices, shards(): lax.all_to_all(computed, ('row', 'col'), split_axis=0, concat_axis=0, til...  4.84 us
    dot_general x1, matrix products, attention(): jnp.einsum('shl,slc->shc', probabilities, latent_cache[:, :, :LATENT], pr...  4.82 us
    pallas_call x1, Pallas kernels, shards(): pl.pallas_call(dispatch_kernel, out_shape=jax.ShapeDtypeStruct((experts,...  3.1 us
    dot_general x1, matrix products, attention(): jnp.einsum('shc,slc->shl', queries, latent_cache, preferred_element_type=...  2.32 us
  transfers between devices with their start and end apart: 1, of which 1 were waited for; matrix products, arithmetic and copies ran while one was open for 9% of the time, Pallas kernels for 0%

profile of v7, /device:TPU:0, one launch (start us, length us, event | category | flops | bytes accessed | tf_op | source)
XLA Modules:
  0.0 91.6 jit_solution(1538911079418456566)
XLA Ops:
  0.6 0.0 copy-start
  0.6 0.9 copy.21
  1.5 0.1 eq.48
  1.6 0.1 convert_compare_fusion
  1.7 0.1 fusion.14
  1.8 0.2 reduce_window_sum.11
  2.0 0.2 select_reduce_fusion
  2.1 0.1 eq.52
  2.2 0.1 and_reduce_fusion
  2.4 0.6 convert_element_type.25.layout_ref
  3.0 3.1 %shard_map.104 = bf16[128,2,3584]{2,1,0:T(2,128)(2,1)} custom-call(bf16[2,16,128]{2,1,0:T(8,128)(2,1)} %convert_element_type.25.layout_ref, bf16[16,3584]{1,0:T(8,128)(2,1)} %hidden_ref.1), custom_call_target="tpu_custom_call" | custom-call | tf_op jit(solution)/shard_map/pallas_call | solution.py:135
  6.1 38.4 %all_to_all.10.rows_ref = bf16[128,2,3584]{2,1,0:T(2,128)(2,1)} all-to-all(bf16[128,2,3584]{2,1,0:T(2,128)(2,1)} %shard_map.104), channel_id=1, replica_groups=mesh['row'=8,'col'=16] {'row','col'}, dimensions={0} | all-to-all | bytes 3670016 | tf_op jit(solution)/shard_map/all_to_all | solution.py:140
  44.5 13.8 %shard_map.105 = bf16[128,2,3584]{2,1,0:T(2,128)(2,1)} custom-call(bf16[128,2,3584]{2,1,0:T(2,128)(2,1)} %all_to_all.10.rows_ref, bf16[1,3584,1024]{2,1,0:T(8,128)(2,1)} %gate_hbm.1, bf16[1,3584,1024]{2,1,0:T(8,128)(2,1)} %up_hbm.1, bf16[1,1024,3584]{2,1,0:T(8,128)(2,1)} %down_hbm.1), custom_call_target="tpu_custom_call" | custom-call | tf_op jit(solution)/shard_map/pallas_call | solution.py:80
  58.3 0.0 copy-start.2
  58.3 0.0 copy-start.3
  58.4 4.8 %all-to-all-start.1 = ((bf16[128,2,3584]{2,1,0:T(2,128)(2,1)}), bf16[128,2,3584]{2,1,0:T(2,128)(2,1)S(1)}, u32[]{:S(2)}, u32[]{:S(2)}) async-start(bf16[128,2,3584]{2,1,0:T(2,128)(2,1)} %shard_map.105), calls=%async_computation.1 | async-start | bytes 3670016 | tf_op jit(solution)/shard_map/all_to_all | solution.py:145
  63.2 0.0 copy-done.2
  63.2 0.1 copy.23
  63.3 0.1 fusion.13
  63.5 0.0 copy-done.3
  63.5 0.1 iota_compare_fusion.3
  63.6 0.0 copy-done
  63.6 2.3 %fusion.11 = f32[16,64,128]{2,1,0:T(8,128)S(1)} fusion(bf16[16,64,576]{2,1,0:T(8,128)(2,1)S(1)} %copy-done, bf16[16,128,576]{1,2,0:T(8,128)(2,1)} %param.16, pred[16,128]{1,0:T(8,128)(4,1)S(1)} %iota_compare_fusion.3), kind=kOutput, calls=%fused_computation.11 | convolution fusion | flops 151257088 | bytes 4065280 | tf_op jit(solution)/shard_map/shc,slc->shl/dot_general | solution.py:16
  65.9 0.0 copy-start.1
  65.9 0.8 copy-done.1
  66.7 0.3 fusion.18
  67.0 4.8 %fusion.5 = bf16[16,64,512]{2,1,0:T(8,128)(2,1)} fusion(bf16[16,128,576]{1,2,0:T(8,128)(2,1)} %param.16, f32[16,64]{1,0:T(8,128)S(1)} %fusion.18, f32[16,64,128]{2,1,0:T(8,128)} %copy-done.1, pred[16,128]{1,0:T(8,128)(4,1)S(1)} %iota_compare_fusion.3), kind=kOutput, calls=%fused_computation.6 | convolution fusion | flops 135267456 | bytes 4200448 | tf_op jit(solution)/shard_map/shl,slc->shc/dot_general | solution.py:26
  71.9 18.3 %all-to-all-done.1 = bf16[128,2,3584]{2,1,0:T(2,128)(2,1)S(1)} async-done(((bf16[128,2,3584]{2,1,0:T(2,128)(2,1)}), bf16[128,2,3584]{2,1,0:T(2,128)(2,1)S(1)}, u32[]{:S(2)}, u32[]{:S(2)}) %all-to-all-start.1) | async-done | bytes 1835040 | tf_op jit(solution)/shard_map/all_to_all | solution.py:145
  90.2 1.5 %fusion.1 = bf16[16,3584]{1,0:T(8,128)(2,1)} fusion(bf16[128,2,3584]{2,1,0:T(2,128)(2,1)S(1)} %all-to-all-done.1, f32[2,16,128]{2,1,0:T(8,128)S(1)} %fusion.13), kind=kOutput, calls=%fused_computation.2 | convolution fusion | flops 176218112 | bytes 1966080 | tf_op jit(solution)/shard_map/dot_general | solution.py:148
  (3 shorter events, 0.0 us)
Async XLA Ops:
  0.6 62.9 %copy-start = (bf16[16,64,576]{2,1,0:T(8,128)(2,1)S(1)}, bf16[16,64,576]{2,1,0:T(8,128)(2,1)}, u32[]{:S(2)}) copy-start(bf16[16,64,576]{2,1,0:T(8,128)(2,1)} %param.15) | copy-start | bytes 3538948
  58.3 4.9 %copy-start.2 = (f32[16,8]{0,1:T(8,128)S(1)}, f32[16,8]{0,1:T(8,128)}, u32[]{:S(2)}) copy-start(f32[16,8]{0,1:T(8,128)} %param.11) | copy-start | bytes 1540
  58.3 5.1 %copy-start.3 = (s32[16]{0:T(128)S(1)}, s32[16]{0:T(128)}, u32[]{:S(2)}) copy-start(s32[16]{0:T(128)} %param.17) | copy-start | bytes 196
  58.4 31.8 %all-to-all-start.1 = ((bf16[128,2,3584]{2,1,0:T(2,128)(2,1)}), bf16[128,2,3584]{2,1,0:T(2,128)(2,1)S(1)}, u32[]{:S(2)}, u32[]{:S(2)}) async-start(bf16[128,2,3584]{2,1,0:T(2,128)(2,1)} %shard_map.105), calls=%async_computation.1 | async-start | bytes 3670016 | tf_op jit(solution)/shard_map/all_to_all | solution.py:145
  65.9 0.8 copy-start.1
